TPU v7x, 32 devices: a whole 2x2x4 slice. The times are simulated.
32 devices in a mesh: bl: 4 (over y, x), freq: 8 (over z, core).
Axes of the slice: x: 2, y: 2, z: 4, core: 2. Of those that a mesh axis runs over, the one named last changes fastest.
Arguments:
- visibility: bfloat16 [2, 64, 1024, 4096], P(None, None, 'freq', 'bl'), may hold values from -6 to 6
- mode_index: int32 [256], replicated, may hold values from 0 to 2047
- beam_mode_weights: bfloat16 [256, 64, 64], replicated, may hold values from -0.75 to 0.75
- inverse_cov: float32 [256, 1024, 1024], P(('bl', 'freq')), may hold values from -2 to 3, as said below
- noise_power: float32 [256, 1024], P(('bl', 'freq')), may hold values from 0.2 to 2
Outputs:
- filtered: float32 [256, 1024, 128], P(('bl', 'freq'))
Inputs may be any that keep to these rules, and one draw needn't show every extreme that they name: Each inverse_cov[m] is symmetric positive definite.
All inputs are finite; a program needn't handle non-finite values.
Results may differ from a plain program's by a relative error of at most 0.0023.
Values may be sent and summed in bfloat16 or wider, within the bound.
No kernel may reach another device: no remote copies, remote signals or barrier semaphores. Data moves between devices by JAX's collectives and lax.ppermute only.
A program may use at most 192 MiB of HBM per device.

v0:
```python
import math

import jax
import jax.numpy as jnp
from jax import lax
from jax.sharding import PartitionSpec as P

CHUNKS = 4


def dft_table(mode_index, sample_ids, length, chunk_count):
    phase_steps = mode_index[None, :] * sample_ids[:, None] % length
    phases = phase_steps.astype(jnp.float32) * (2.0 * math.pi / length)
    norming = 1.0 / math.sqrt(length)
    cosine = (jnp.cos(phases) * norming).reshape(sample_ids.shape[0], chunk_count, 1, -1)
    sine_part = (jnp.sin(phases) * norming).reshape(sample_ids.shape[0], chunk_count, 1, -1)
    real_rows = jnp.concatenate([cosine, -sine_part], axis=2)
    imag_rows = jnp.concatenate([sine_part, cosine], axis=2)
    table = jnp.stack([real_rows, imag_rows]).astype(jnp.bfloat16)
    return table.reshape(2, sample_ids.shape[0], -1)


def transform(samples, dft_weights):
    return lax.dot_general(
        samples, dft_weights, (((0, 3), (0, 1)), ((), ())), preferred_element_type=jnp.float32
    )


def project(spectrum, beam_rows):
    row_count, freq_count, column_total = spectrum.shape
    mode_count = column_total // 2
    halves = spectrum.reshape(row_count, freq_count, 2, mode_count)
    high = lax.reduce_precision(halves, exponent_bits=8, mantissa_bits=7)
    low = (halves - high).astype(jnp.bfloat16)
    high = high.astype(jnp.bfloat16)
    dims = (((0,), (2,)), ((3,), (0,)))
    projected = lax.dot_general(high, beam_rows, dims, preferred_element_type=jnp.float32)
    projected = projected + lax.dot_general(low, beam_rows, dims, preferred_element_type=jnp.float32)
    return projected.reshape(mode_count, freq_count, 2 * beam_rows.shape[1])


def reduce_over_bl(partial, bl_devices):
    bits = bl_devices.bit_length() - 1
    if bits == 0 or (1 << bits) != bl_devices or partial.shape[1] % 2:
        return lax.psum_scatter(partial, "bl", scatter_dimension=0, tiled=True)
    me = lax.axis_index("bl")
    rows, freq_count = partial.shape[0], partial.shape[1]
    grid = partial.reshape((2,) * bits + (rows // bl_devices,) + partial.shape[1:])
    half = freq_count // 2
    parts = [grid[..., :half, :], grid[..., half:, :]]
    orders = [list(range(bits)), list(reversed(range(bits)))]
    axis_bits = [[bits - 1 - a for a in range(bits)] for _ in parts]
    for step in range(bits):
        for p in range(len(parts)):
            bit = orders[p][step]
            axis = axis_bits[p].index(bit)
            mine = (me >> bit) & 1
            keep = lax.dynamic_index_in_dim(parts[p], mine, axis, keepdims=False)
            send = lax.dynamic_index_in_dim(parts[p], 1 - mine, axis, keepdims=False)
            pairs = [(q, q ^ (1 << bit)) for q in range(bl_devices)]
            parts[p] = keep + lax.ppermute(send, "bl", perm=pairs)
            axis_bits[p].pop(axis)
    return jnp.concatenate(parts, axis=1)


def weigh_all(inverse_cov, noise_power, owner_modes):
    weighted = jnp.einsum("mfg,mgk->mfk", inverse_cov, owner_modes, precision=lax.Precision.HIGH)
    return owner_modes - noise_power[:, :, None] * weighted


def body(visibility, mode_index, beam_mode_weights, inverse_cov, noise_power):
    bl_devices = lax.axis_size("bl")
    freq_devices = lax.axis_size("freq")
    local_times = visibility.shape[3]
    total_times = local_times * bl_devices
    owned = inverse_cov.shape[0]
    chunk_count = math.gcd(CHUNKS, owned)
    chunk = owned // chunk_count
    sample_ids = lax.axis_index("bl") * local_times + jnp.arange(local_times, dtype=jnp.int32)
    index_grid = mode_index.reshape(bl_devices, freq_devices, chunk_count, chunk)
    ordered_modes = jnp.transpose(index_grid, (2, 0, 1, 3)).reshape(-1)
    beam_tail = beam_mode_weights.shape[1:]
    beam_grid = beam_mode_weights.reshape((bl_devices, freq_devices, chunk_count, chunk) + beam_tail)
    dft_weights = dft_table(ordered_modes, sample_ids, total_times, chunk_count)
    spectrum = transform(visibility, dft_weights)
    width = spectrum.shape[2] // chunk_count
    pieces = []
    for step in range(chunk_count):
        beams = beam_grid[:, :, step].reshape((-1,) + beam_tail)
        partial_terms = project(spectrum[:, :, step * width:(step + 1) * width], beams)
        summed_modes = reduce_over_bl(partial_terms, bl_devices)
        owner_modes = lax.all_to_all(summed_modes, "freq", split_axis=0, concat_axis=1, tiled=True)
        lo = step * chunk
        pieces.append(
            weigh_all(inverse_cov[lo:lo + chunk], noise_power[lo:lo + chunk], owner_modes)
        )
    return jnp.concatenate(pieces, axis=0)


def solution(mesh):
    placed = (
        P(None, None, "freq", "bl"),
        P(),
        P(),
        P(("bl", "freq"), None, None),
        P(("bl", "freq"), None),
    )
    return jax.shard_map(
        body, mesh=mesh, in_specs=placed, out_specs=P(("bl", "freq"), None, None), check_vma=False
    )
```

profile of v0, /device:TPU:0, one launch (start us, length us, event | category | flops | bytes accessed | tf_op | source)
XLA Modules:
  0.0 359.1 jit_solution(1622108234412760629)
XLA Ops:
  1.2 4.6 %negate_convert_fusion = (bf16[1024,4,1,64]{0,3,2,1:T(8,128)(2,1)S(1)}, bf16[1024,4,1,64]{0,3,2,1:T(8,128)(2,1)S(1)}, bf16[1024,4,1,64]{0,3,2,1:T(8,128)(2,1)S(1)}) fusion(s32[1024]{0:T(1024)S(1)} %iota_add_fusion, s32[4,64]{1,0:T(4,128)S(1)} %copy.38), kind=kLoop, calls=%fused_computation.68 | loop fusion | flops 5242880 | bytes 1577984 | tf_op jit(solution)/shard_map/convert.7
  6.0 24.0 %convolution_bitcast_fusion = f32[64,128,512]{1,2,0:T(8,128)} fusion(bf16[2,64,128,1024]{3,2,1,0:T(8,128)(2,1)} %param.5, bf16[1,1024,512]{1,2,0:T(8,128)(2,1)S(1)} %bitcast.185, bf16[1,1024,512]{1,2,0:T(8,128)(2,1)S(1)} %bitcast.184), kind=kOutput, calls=%fused_computation | convolution fusion | flops 17184063488 | bytes 52428800 | tf_op jit(solution)/shard_map/dot_general | solution.py:24
  30.0 12.5 %fusion.65 = (f32[64,128,128]{1,2,0:T(8,128)}, f32[64,128,128]{1,2,0:T(8,128)}, f32[64,128,128]{1,2,0:T(8,128)}, f32[64,128,128]{1,2,0:T(8,128)}) fusion(f32[64,128,512]{1,2,0:T(8,128)} %convolution_bitcast_fusion), kind=kLoop, calls=%fused_computation.106 | loop fusion | bytes 33554432 | tf_op jit(solution)/shard_map/slice | solution.py:90
  42.5 6.8 %copy.41 = bf16[256,64,64]{2,1,0:T(8,128)(2,1)} copy(bf16[256,64,64]{0,2,1:T(8,128)(2,1)S(1)} %copy-done.13) | data formatting | bytes 4194304 | tf_op args[2]
  49.3 3.7 %fusion.67 = (bf16[4,8,1,2,64,64]{5,4,3,2,1,0:T(8,128)(2,1)S(1)}, bf16[4,8,1,2,64,64]{5,4,3,2,1,0:T(8,128)(2,1)S(1)}, bf16[4,8,1,2,64,64]{5,4,3,2,1,0:T(8,128)(2,1)S(1)}, bf16[4,8,1,2,64,64]{5,4,3,2,1,0:T(8,128)(2,1)S(1)}) fusion(bf16[4,8,4,2,64,64]{5,4,3,2,1,0:T(8,128)(2,1)} %bitcast.170), kind=kLoop, calls=%fused_computation.108 | loop fusion | bytes 4194304 | tf_op jit(solution)/shard_map/slice | solution.py:89
  53.0 2.8 fusion.16
  55.8 2.7 convolution_add_fusion.3
  58.4 4.9 %fusion.66 = (f32[2,2,16,64,128]{3,4,2,1,0:T(8,128)}, f32[2,2,16,64,128]{3,4,2,1,0:T(8,128)}) fusion(f32[2,2,16,128,128]{3,4,2,1,0:T(8,128)S(1)} %bitcast.159), kind=kLoop, calls=%fused_computation.107 | loop fusion | bytes 8388608 | tf_op jit(solution)/shard_map/slice | solution.py:50
  63.4 4.8 %constant_dynamic-slice_fusion.15 = (f32[2,1,16,64,128]{3,4,2,1,0:T(8,128)}, f32[2,1,16,64,128]{3,4,2,1,0:T(8,128)}) fusion(f32[2,2,16,64,128]{3,4,2,1,0:T(8,128)} %get-tuple-element.11, s32[]{:T(128)S(6)} %select_n.67, s32[]{:T(128)S(6)} %select_n.68), kind=kLoop, calls=%fused_computation.103 | loop fusion | bytes 4194312 | tf_op jit(solution)/shard_map/jit(dynamic_index_in_dim)/dynamic_slice | solution.py:58
  68.2 3.2 copy.69
  71.3 2.9 collective-permute-start
  74.3 4.7 %constant_dynamic-slice_fusion.13 = (f32[1,2,16,64,128]{3,4,2,1,0:T(8,128)}, f32[1,2,16,64,128]{3,4,2,1,0:T(8,128)}) fusion(f32[2,2,16,64,128]{3,4,2,1,0:T(8,128)} %get-tuple-element.12, s32[]{:T(128)S(6)} %select_n.69, s32[]{:T(128)S(6)} %select_n.70), kind=kLoop, calls=%fused_computation.101 | loop fusion | bytes 4194312 | tf_op jit(solution)/shard_map/jit(dynamic_index_in_dim)/dynamic_slice | solution.py:58
  79.0 3.2 copy.72
  83.7 5.1 %fusion.17 = f32[64,128,2,64]{1,3,2,0:T(8,128)S(1)} fusion(bf16[64,64,64,1]{2,1,3,0:T(8,128)(2,1)S(1)} %bitcast.175, f32[64,128,2,64]{1,3,2,0:T(8,128)} %bitcast.166), kind=kOutput, calls=%fused_computation.27 | convolution fusion | flops 136314880 | bytes 8912896 | tf_op jit(solution)/shard_map/dot_general | solution.py:37
  88.8 3.1 convolution_add_fusion.2
  91.9 3.8 %fusion.68 = (f32[2,2,16,64,128]{3,4,2,1,0:T(8,128)S(1)}, f32[2,2,16,64,128]{3,4,2,1,0:T(8,128)}) fusion(f32[2,2,16,128,128]{3,4,2,1,0:T(8,128)S(1)} %bitcast.160), kind=kLoop, calls=%fused_computation.109 | loop fusion | bytes 8388608 | tf_op jit(solution)/shard_map/slice | solution.py:50
  95.7 2.3 constant_dynamic-slice_fusion.11
  98.0 3.2 copy.75
  101.7 4.8 %constant_dynamic-slice_fusion.9 = (f32[1,2,16,64,128]{3,4,2,1,0:T(8,128)}, f32[1,2,16,64,128]{3,4,2,1,0:T(8,128)}) fusion(f32[2,2,16,64,128]{3,4,2,1,0:T(8,128)} %get-tuple-element.22, s32[]{:T(128)S(6)} %select_n.69, s32[]{:T(128)S(6)} %select_n.70), kind=kLoop, calls=%fused_computation.97 | loop fusion | bytes 4194312 | tf_op jit(solution)/shard_map/jit(dynamic_index_in_dim)/dynamic_slice | solution.py:58
  106.5 3.1 copy.78
  109.6 5.1 %fusion.18 = f32[64,128,2,64]{1,3,2,0:T(8,128)S(1)} fusion(bf16[64,64,64,1]{2,1,3,0:T(8,128)(2,1)S(1)} %bitcast.173, f32[64,128,2,64]{1,3,2,0:T(8,128)} %bitcast.164), kind=kOutput, calls=%fused_computation.28 | convolution fusion | flops 136314880 | bytes 8912896 | tf_op jit(solution)/shard_map/dot_general | solution.py:37
  114.7 2.7 convolution_add_fusion.1
  117.4 3.7 %fusion.69 = (f32[2,2,16,64,128]{3,4,2,1,0:T(8,128)S(1)}, f32[2,2,16,64,128]{3,4,2,1,0:T(8,128)}) fusion(f32[2,2,16,128,128]{3,4,2,1,0:T(8,128)S(1)} %bitcast.161), kind=kLoop, calls=%fused_computation.110 | loop fusion | bytes 8388608 | tf_op jit(solution)/shard_map/slice | solution.py:50
  121.1 1.9 constant_dynamic-slice_fusion.7
  123.0 3.2 copy.81
  126.2 2.0 collective-permute-start.8
  128.2 3.1 copy.68
  131.3 3.1 copy.71
  134.4 5.1 %fusion.19 = f32[64,128,2,64]{1,3,2,0:T(8,128)S(1)} fusion(bf16[64,64,64,1]{2,1,3,0:T(8,128)(2,1)S(1)} %bitcast.171, f32[64,128,2,64]{1,3,2,0:T(8,128)} %bitcast.162), kind=kOutput, calls=%fused_computation.29 | convolution fusion | flops 136314880 | bytes 8912896 | tf_op jit(solution)/shard_map/dot_general | solution.py:37
  146.6 4.7 %convolution_add_fusion = f32[64,128,2,64]{1,3,2,0:T(8,128)} fusion(f32[64,128,2,64]{1,3,2,0:T(8,128)S(1)} %fusion.19, bf16[64,64,64,1]{2,1,3,0:T(8,128)(2,1)S(1)} %bitcast.172, f32[64,128,2,64]{1,3,2,0:T(8,128)S(1)} %bitcast.163), kind=kOutput, calls=%fused_computation.22 | convolution fusion | flops 138412032 | bytes 13107200 | tf_op jit(solution)/shard_map/dot_general | solution.py:38
  151.3 3.2 copy.74
  154.5 2.2 copy.77
  156.7 4.7 %constant_dynamic-slice_fusion.5 = (f32[1,2,16,64,128]{3,4,2,1,0:T(8,128)}, f32[1,2,16,64,128]{3,4,2,1,0:T(8,128)}) fusion(f32[2,2,16,64,128]{3,4,2,1,0:T(8,128)} %get-tuple-element.28, s32[]{:T(128)S(6)} %select_n.69, s32[]{:T(128)S(6)} %select_n.70), kind=kLoop, calls=%fused_computation.93 | loop fusion | bytes 4194312 | tf_op jit(solution)/shard_map/jit(dynamic_index_in_dim)/dynamic_slice | solution.py:58
  161.4 3.2 copy.84
  168.2 5.4 %all-to-all-start = ((f32[16,128,128]{2,1,0:T(8,128)}), f32[16,128,128]{2,1,0:T(8,128)}, u32[]{:S(2)}, u32[]{:S(2)}) async-start(f32[16,128,128]{2,1,0:T(8,128)} %pad_maximum_fusion.3), calls=%async_computation | async-start | bytes 2097152 | tf_op jit(solution)/shard_map/all_to_all | solution.py:92
  173.6 1.8 bitcast_add_fusion.5
  180.1 4.9 %fusion.70 = (f32[2,2,16,64,128]{3,4,2,1,0:T(8,128)}, f32[2,2,16,64,128]{3,4,2,1,0:T(8,128)}) fusion(f32[2,2,16,128,128]{3,4,2,1,0:T(8,128)S(1)} %bitcast.158), kind=kLoop, calls=%fused_computation.111 | loop fusion | bytes 8388608 | tf_op jit(solution)/shard_map/slice | solution.py:50
  185.0 14.0 %collective-permute-done.5 = f32[16,64,128]{2,1,0:T(8,128)S(1)} collective-permute-done((f32[16,64,128]{2,1,0:T(8,128)S(1)}, f32[16,64,128]{2,1,0:T(8,128)S(1)}, u32[]{:S(2)}, u32[]{:S(2)}) %collective-permute-start.5) | collective-permute-done | bytes 524320 | tf_op jit(solution)/shard_map/ppermute | solution.py:61
  200.3 4.8 %all-to-all-start.1 = ((f32[16,128,128]{2,1,0:T(8,128)}), f32[16,128,128]{2,1,0:T(8,128)}, u32[]{:S(2)}, u32[]{:S(2)}) async-start(f32[16,128,128]{2,1,0:T(8,128)} %pad_maximum_fusion.4), calls=%async_computation.1 | async-start | bytes 2097152 | tf_op jit(solution)/shard_map/all_to_all | solution.py:92
  205.1 4.8 %constant_dynamic-slice_fusion.3 = (f32[2,1,16,64,128]{3,4,2,1,0:T(8,128)}, f32[2,1,16,64,128]{3,4,2,1,0:T(8,128)}) fusion(f32[2,2,16,64,128]{3,4,2,1,0:T(8,128)} %get-tuple-element.33, s32[]{:T(128)S(6)} %select_n.67, s32[]{:T(128)S(6)} %select_n.68), kind=kLoop, calls=%fused_computation.91 | loop fusion | bytes 4194312 | tf_op jit(solution)/shard_map/jit(dynamic_index_in_dim)/dynamic_slice | solution.py:58
  209.9 3.2 copy.87
  216.1 2.2 copy.83
  218.3 1.8 bitcast_add_fusion.3
  224.8 1.7 constant_dynamic-slice_fusion.1
  229.1 7.0 %collective-permute-done.9 = f32[16,64,128]{2,1,0:T(8,128)} collective-permute-done((f32[16,64,128]{2,1,0:T(8,128)}, f32[16,64,128]{2,1,0:T(8,128)}, u32[]{:S(2)}, u32[]{:S(2)}) %collective-permute-start.9) | collective-permute-done | bytes 524320 | tf_op jit(solution)/shard_map/ppermute | solution.py:61
  237.2 13.0 %collective-permute-done.11 = f32[16,64,128]{2,1,0:T(8,128)} collective-permute-done((f32[16,64,128]{2,1,0:T(8,128)}, f32[16,64,128]{2,1,0:T(8,128)}, u32[]{:S(2)}, u32[]{:S(2)}) %collective-permute-start.11) | collective-permute-done | bytes 524320 | tf_op jit(solution)/shard_map/ppermute | solution.py:61
  252.5 4.7 %all-to-all-start.2 = ((f32[16,128,128]{2,1,0:T(8,128)}), f32[16,128,128]{2,1,0:T(8,128)}, u32[]{:S(2)}, u32[]{:S(2)}) async-start(f32[16,128,128]{2,1,0:T(8,128)} %pad_maximum_fusion.5), calls=%async_computation.2 | async-start | bytes 2097152 | tf_op jit(solution)/shard_map/all_to_all | solution.py:92
  257.9 2.2 copy.89
  265.4 10.5 %collective-permute-done.13 = f32[16,64,128]{2,1,0:T(8,128)S(1)} collective-permute-done((f32[16,64,128]{2,1,0:T(8,128)S(1)}, f32[16,64,128]{2,1,0:T(8,128)S(1)}, u32[]{:S(2)}, u32[]{:S(2)}) %collective-permute-start.13) | collective-permute-done | bytes 524320 | tf_op jit(solution)/shard_map/ppermute | solution.py:61
  276.0 2.0 collective-permute-done.15
  279.1 4.9 %all-to-all-done.2 = f32[16,128,128]{2,1,0:T(8,128)} async-done(((f32[16,128,128]{2,1,0:T(8,128)}), f32[16,128,128]{2,1,0:T(8,128)}, u32[]{:S(2)}, u32[]{:S(2)}) %all-to-all-start.2) | async-done | bytes 1048608 | tf_op jit(solution)/shard_map/all_to_all | solution.py:92
  284.0 4.5 %all-to-all-start.3 = ((f32[16,128,128]{2,1,0:T(8,128)}), f32[16,128,128]{2,1,0:T(8,128)}, u32[]{:S(2)}, u32[]{:S(2)}) async-start(f32[16,128,128]{2,1,0:T(8,128)} %pad_maximum_fusion.6), calls=%async_computation.3 | async-start | bytes 2097152 | tf_op jit(solution)/shard_map/all_to_all | solution.py:92
  288.5 1.6 copy.45
  290.3 1.6 copy.50
  292.1 2.6 copy.55
  296.0 18.8 %all-to-all-done.3 = f32[16,128,128]{2,1,0:T(8,128)} async-done(((f32[16,128,128]{2,1,0:T(8,128)}), f32[16,128,128]{2,1,0:T(8,128)}, u32[]{:S(2)}, u32[]{:S(2)}) %all-to-all-start.3) | async-done | bytes 1048608 | tf_op jit(solution)/shard_map/all_to_all | solution.py:92
  314.8 2.5 copy.60
  317.4 2.4 all_to_all.67
  319.8 7.6 %fusion.30 = f32[2,1024,128]{1,2,0:T(8,128)S(1)} fusion(f32[2,1024,128]{1,2,0:T(8,128)S(1)} %all_to_all.55, f32[8,1024,1024]{2,1,0:T(8,128)} %param.8, f32[2,1024]{1,0:T(2,128)S(1)} %get-tuple-element.39), kind=kOutput, calls=%fused_computation.41 | convolution fusion | flops 1611137024 | bytes 11542528 | tf_op jit(solution)/shard_map/mfg,mgk->mfk/dot_general | solution.py:67
  327.4 7.6 %fusion.39 = f32[2,1024,128]{1,2,0:T(8,128)S(1)} fusion(f32[2,1024,128]{1,2,0:T(8,128)S(1)} %all_to_all.59, f32[8,1024,1024]{2,1,0:T(8,128)} %param.8, f32[2,1024]{1,0:T(2,128)S(1)} %get-tuple-element.40), kind=kOutput, calls=%fused_computation.44 | convolution fusion | flops 1611137024 | bytes 11542528 | tf_op jit(solution)/shard_map/mfg,mgk->mfk/dot_general | solution.py:67
  335.1 7.7 %fusion.48 = f32[2,1024,128]{1,2,0:T(8,128)S(1)} fusion(f32[2,1024,128]{1,2,0:T(8,128)S(1)} %all_to_all.63, f32[8,1024,1024]{2,1,0:T(8,128)} %param.8, f32[2,1024]{1,0:T(2,128)S(1)} %get-tuple-element.42), kind=kOutput, calls=%fused_computation.47 | convolution fusion | flops 1611137024 | bytes 11542528 | tf_op jit(solution)/shard_map/mfg,mgk->mfk/dot_general | solution.py:67
  342.8 8.0 %fusion.57 = f32[2,1024,128]{1,2,0:T(8,128)S(1)} fusion(f32[2,1024,128]{1,2,0:T(8,128)S(1)} %copy-done.12, f32[8,1024,1024]{2,1,0:T(8,128)} %param.8, f32[2,1024]{1,0:T(2,128)S(1)} %get-tuple-element.41), kind=kOutput, calls=%fused_computation.50 | convolution fusion | flops 1611137024 | bytes 11542528 | tf_op jit(solution)/shard_map/mfg,mgk->mfk/dot_general | solution.py:67
  350.8 2.6 pad_maximum_fusion
  353.4 5.3 %copy.61 = f32[8,1024,128]{2,1,0:T(8,128)} copy(f32[8,1024,128]{1,2,0:T(8,128)} %pad_maximum_fusion) | data formatting | bytes 8388608 | tf_op jit(solution)/shard_map/concatenate | solution.py:97
  (95 shorter events, 42.4 us)
Async XLA Ops:
  29.9 12.5 %copy-start.13 = (bf16[256,64,64]{0,2,1:T(8,128)(2,1)S(1)}, bf16[256,64,64]{0,2,1:T(8,128)(2,1)}, u32[]{:S(2)}) copy-start(bf16[256,64,64]{0,2,1:T(8,128)(2,1)} %param.7) | copy-start | bytes 6291460
  49.3 3.7 %copy-start.4 = (f32[64,128,128]{1,2,0:T(8,128)S(1)}, f32[64,128,128]{1,2,0:T(8,128)}, u32[]{:S(2)}) copy-start(f32[64,128,128]{1,2,0:T(8,128)} %get-tuple-element.5) | copy-start | bytes 12582916
  71.3 68.2 %collective-permute-start = (f32[2,16,64,128]{3,2,1,0:T(8,128)}, f32[2,16,64,128]{3,2,1,0:T(8,128)}, u32[]{:S(2)}, u32[]{:S(2)}) collective-permute-start(f32[2,16,64,128]{3,2,1,0:T(8,128)} %bitcast.181), channel_id=1, source_target_pairs={{0,8},{8,0},{16,24},{24,16},{1,9},{9,1},{17,25},{25,17},{2,10},{10... | collective-permute-start | bytes 3145736 | tf_op jit(solution)/shard_map/ppermute | solution.py:61
  82.2 61.4 %collective-permute-start.2 = (f32[2,16,64,128]{3,2,1,0:T(8,128)}, f32[2,16,64,128]{3,2,1,0:T(8,128)}, u32[]{:S(2)}, u32[]{:S(2)}) collective-permute-start(f32[2,16,64,128]{3,2,1,0:T(8,128)} %bitcast.182), channel_id=1, source_target_pairs={{0,16},{8,24},{16,0},{24,8},{1,17},{9,25},{17,1},{25,9},{2,18},{10... | collective-permute-start | bytes 3145736 | tf_op jit(solution)/shard_map/ppermute | solution.py:61
  83.7 5.1 %copy-start.3 = (f32[64,128,128]{1,2,0:T(8,128)S(1)}, f32[64,128,128]{1,2,0:T(8,128)}, u32[]{:S(2)}) copy-start(f32[64,128,128]{1,2,0:T(8,128)} %get-tuple-element.8) | copy-start | bytes 12582916
  101.2 72.5 %collective-permute-start.4 = (f32[2,16,64,128]{3,2,1,0:T(8,128)}, f32[2,16,64,128]{3,2,1,0:T(8,128)}, u32[]{:S(2)}, u32[]{:S(2)}) collective-permute-start(f32[2,16,64,128]{3,2,1,0:T(8,128)} %bitcast.36), channel_id=1, source_target_pairs={{0,8},{8,0},{16,24},{24,16},{1,9},{9,1},{17,25},{25,17},{2,10},{10... | collective-permute-start | bytes 3145736 | tf_op jit(solution)/shard_map/ppermute | solution.py:61
  109.6 67.5 %collective-permute-start.6 = (f32[2,16,64,128]{3,2,1,0:T(8,128)}, f32[2,16,64,128]{3,2,1,0:T(8,128)}, u32[]{:S(2)}, u32[]{:S(2)}) collective-permute-start(f32[2,16,64,128]{3,2,1,0:T(8,128)} %bitcast.40), channel_id=1, source_target_pairs={{0,16},{8,24},{16,0},{24,8},{1,17},{9,25},{17,1},{25,9},{2,18},{10... | collective-permute-start | bytes 3145736 | tf_op jit(solution)/shard_map/ppermute | solution.py:61
  109.6 5.1 %copy-start.2 = (f32[64,128,128]{1,2,0:T(8,128)S(1)}, f32[64,128,128]{1,2,0:T(8,128)}, u32[]{:S(2)}) copy-start(f32[64,128,128]{1,2,0:T(8,128)} %get-tuple-element.7) | copy-start | bytes 12582916
  126.2 92.2 %collective-permute-start.8 = (f32[2,16,64,128]{3,2,1,0:T(8,128)}, f32[2,16,64,128]{3,2,1,0:T(8,128)}, u32[]{:S(2)}, u32[]{:S(2)}) collective-permute-start(f32[2,16,64,128]{3,2,1,0:T(8,128)} %bitcast.179), channel_id=1, source_target_pairs={{0,8},{8,0},{16,24},{24,16},{1,9},{9,1},{17,25},{25,17},{2,10},{10... | collective-permute-start | bytes 3145736 | tf_op jit(solution)/shard_map/ppermute | solution.py:61
  134.4 5.1 %copy-start.8 = (f32[2,1,16,64,128]{4,3,2,0,1:T(8,128)S(1)}, f32[2,1,16,64,128]{4,3,2,0,1:T(8,128)}, u32[]{:S(2)}) copy-start(f32[2,1,16,64,128]{4,3,2,0,1:T(8,128)} %copy.68) | copy-start | bytes 3145732
  134.4 9.1 %copy-start.7 = (f32[1,2,16,64,128]{4,3,2,1,0:T(8,128)S(1)}, f32[1,2,16,64,128]{4,3,2,1,0:T(8,128)}, u32[]{:S(2)}) copy-start(f32[1,2,16,64,128]{4,3,2,1,0:T(8,128)} %copy.71) | copy-start | bytes 3145732
  139.6 7.1 %copy-start.1 = (f32[64,128,128]{1,2,0:T(8,128)S(1)}, f32[64,128,128]{1,2,0:T(8,128)}, u32[]{:S(2)}) copy-start(f32[64,128,128]{1,2,0:T(8,128)} %get-tuple-element.6) | copy-start | bytes 12582916
  141.1 3.8 %copy-start.9 = (f32[2,16,64,128]{3,2,1,0:T(8,128)}, f32[2,16,64,128]{3,2,1,0:T(8,128)S(1)}, u32[]{:S(2)}) copy-start(f32[2,16,64,128]{3,2,1,0:T(8,128)S(1)} %bitcast_add_fusion.7) | copy-start | bytes 3145732
  142.0 22.6 %collective-permute-start.1 = (f32[16,64,128]{2,1,0:T(8,128)}, f32[16,64,128]{2,1,0:T(8,128)}, u32[]{:S(2)}, u32[]{:S(2)}) collective-permute-start(f32[16,64,128]{2,1,0:T(8,128)} %dynamic-slice_bitcast_fusion.7), channel_id=1, source_target_pairs={{0,16},{8,24},{16,0},{24,8},{1,17},{9,25},{17,1},{25,9},{2,18},{10... | collective-permute-start | bytes 1572872 | tf_op jit(solution)/shard_map/ppermute | solution.py:61
  145.0 1.1 copy-start.10
  146.1 19.8 %collective-permute-start.3 = (f32[16,64,128]{2,1,0:T(8,128)}, f32[16,64,128]{2,1,0:T(8,128)}, u32[]{:S(2)}, u32[]{:S(2)}) collective-permute-start(f32[16,64,128]{2,1,0:T(8,128)} %dynamic-slice_bitcast_fusion.6), channel_id=1, source_target_pairs={{0,8},{8,0},{16,24},{24,16},{1,9},{9,1},{17,25},{25,17},{2,10},{10... | collective-permute-start | bytes 1572872 | tf_op jit(solution)/shard_map/ppermute | solution.py:61
  164.6 57.3 %collective-permute-start.10 = (f32[2,16,64,128]{3,2,1,0:T(8,128)}, f32[2,16,64,128]{3,2,1,0:T(8,128)}, u32[]{:S(2)}, u32[]{:S(2)}) collective-permute-start(f32[2,16,64,128]{3,2,1,0:T(8,128)} %bitcast.180), channel_id=1, source_target_pairs={{0,16},{8,24},{16,0},{24,8},{1,17},{9,25},{17,1},{25,9},{2,18},{10... | collective-permute-start | bytes 3145736 | tf_op jit(solution)/shard_map/ppermute | solution.py:61
  168.2 32.1 %all-to-all-start = ((f32[16,128,128]{2,1,0:T(8,128)}), f32[16,128,128]{2,1,0:T(8,128)}, u32[]{:S(2)}, u32[]{:S(2)}) async-start(f32[16,128,128]{2,1,0:T(8,128)} %pad_maximum_fusion.3), calls=%async_computation | async-start | bytes 2097152 | tf_op jit(solution)/shard_map/all_to_all | solution.py:92
  173.6 6.5 %copy-start = (f32[64,128,2,64]{1,3,2,0:T(8,128)S(1)}, f32[64,128,2,64]{1,3,2,0:T(8,128)}, u32[]{:S(2)}) copy-start(f32[64,128,2,64]{1,3,2,0:T(8,128)} %convolution_add_fusion) | copy-start | bytes 12582916
  175.5 23.5 %collective-permute-start.5 = (f32[16,64,128]{2,1,0:T(8,128)S(1)}, f32[16,64,128]{2,1,0:T(8,128)S(1)}, u32[]{:S(2)}, u32[]{:S(2)}) collective-permute-start(f32[16,64,128]{2,1,0:T(8,128)S(1)} %dynamic-slice_bitcast_fusion.5), channel_id=1, source_target_pairs={{0,16},{8,24},{16,0},{24,8},{1,17},{9,25},{17,1},{25,9},{2,18},{10... | collective-permute-start | bytes 1572872 | tf_op jit(solution)/shard_map/ppermute | solution.py:61
  178.5 20.6 %collective-permute-start.7 = (f32[16,64,128]{2,1,0:T(8,128)S(1)}, f32[16,64,128]{2,1,0:T(8,128)S(1)}, u32[]{:S(2)}, u32[]{:S(2)}) collective-permute-start(f32[16,64,128]{2,1,0:T(8,128)S(1)} %dynamic-slice_bitcast_fusion.4), channel_id=1, source_target_pairs={{0,8},{8,0},{16,24},{24,16},{1,9},{9,1},{17,25},{25,17},{2,10},{10... | collective-permute-start | bytes 1572872 | tf_op jit(solution)/shard_map/ppermute | solution.py:61
  200.3 52.2 %all-to-all-start.1 = ((f32[16,128,128]{2,1,0:T(8,128)}), f32[16,128,128]{2,1,0:T(8,128)}, u32[]{:S(2)}, u32[]{:S(2)}) async-start(f32[16,128,128]{2,1,0:T(8,128)} %pad_maximum_fusion.4), calls=%async_computation.1 | async-start | bytes 2097152 | tf_op jit(solution)/shard_map/all_to_all | solution.py:92
  213.1 47.0 %collective-permute-start.12 = (f32[2,16,64,128]{3,2,1,0:T(8,128)}, f32[2,16,64,128]{3,2,1,0:T(8,128)}, u32[]{:S(2)}, u32[]{:S(2)}) collective-permute-start(f32[2,16,64,128]{3,2,1,0:T(8,128)} %bitcast.72), channel_id=1, source_target_pairs={{0,8},{8,0},{16,24},{24,16},{1,9},{9,1},{17,25},{25,17},{2,10},{10... | collective-permute-start | bytes 3145736 | tf_op jit(solution)/shard_map/ppermute | solution.py:61
  218.3 6.5 %copy-start.5 = (f32[2,2,16,64,128]{3,4,2,1,0:T(8,128)S(1)}, f32[2,2,16,64,128]{3,4,2,1,0:T(8,128)}, u32[]{:S(2)}) copy-start(f32[2,2,16,64,128]{3,4,2,1,0:T(8,128)} %get-tuple-element.34) | copy-start | bytes 6291460
  221.0 15.1 %collective-permute-start.9 = (f32[16,64,128]{2,1,0:T(8,128)}, f32[16,64,128]{2,1,0:T(8,128)}, u32[]{:S(2)}, u32[]{:S(2)}) collective-permute-start(f32[16,64,128]{2,1,0:T(8,128)} %dynamic-slice_bitcast_fusion.3), channel_id=1, source_target_pairs={{0,16},{8,24},{16,0},{24,8},{1,17},{9,25},{17,1},{25,9},{2,18},{10... | collective-permute-start | bytes 1572872 | tf_op jit(solution)/shard_map/ppermute | solution.py:61
  223.3 1.4 copy-start.11
  224.3 25.9 %collective-permute-start.11 = (f32[16,64,128]{2,1,0:T(8,128)}, f32[16,64,128]{2,1,0:T(8,128)}, u32[]{:S(2)}, u32[]{:S(2)}) collective-permute-start(f32[16,64,128]{2,1,0:T(8,128)} %dynamic-slice_bitcast_fusion.2), channel_id=1, source_target_pairs={{0,8},{8,0},{16,24},{24,16},{1,9},{9,1},{17,25},{25,17},{2,10},{10... | collective-permute-start | bytes 1572872 | tf_op jit(solution)/shard_map/ppermute | solution.py:61
  228.0 29.2 %copy-start.6 = (f32[2,1,16,64,128]{3,4,2,1,0:T(8,128)S(1)}, f32[2,1,16,64,128]{3,4,2,1,0:T(8,128)}, u32[]{:S(2)}) copy-start(f32[2,1,16,64,128]{3,4,2,1,0:T(8,128)} %get-tuple-element.31) | copy-start | bytes 3145732
  228.0 34.4 %collective-permute-start.14 = (f32[2,16,64,128]{3,2,1,0:T(8,128)}, f32[2,16,64,128]{3,2,1,0:T(8,128)}, u32[]{:S(2)}, u32[]{:S(2)}) collective-permute-start(f32[2,16,64,128]{3,2,1,0:T(8,128)} %bitcast.183), channel_id=1, source_target_pairs={{0,16},{8,24},{16,0},{24,8},{1,17},{9,25},{17,1},{25,9},{2,18},{10... | collective-permute-start | bytes 3145736 | tf_op jit(solution)/shard_map/ppermute | solution.py:61
  252.5 31.4 %all-to-all-start.2 = ((f32[16,128,128]{2,1,0:T(8,128)}), f32[16,128,128]{2,1,0:T(8,128)}, u32[]{:S(2)}, u32[]{:S(2)}) async-start(f32[16,128,128]{2,1,0:T(8,128)} %pad_maximum_fusion.5), calls=%async_computation.2 | async-start | bytes 2097152 | tf_op jit(solution)/shard_map/all_to_all | solution.py:92
  261.5 14.4 %collective-permute-start.13 = (f32[16,64,128]{2,1,0:T(8,128)S(1)}, f32[16,64,128]{2,1,0:T(8,128)S(1)}, u32[]{:S(2)}, u32[]{:S(2)}) collective-permute-start(f32[16,64,128]{2,1,0:T(8,128)S(1)} %dynamic-slice_bitcast_fusion.1), channel_id=1, source_target_pairs={{0,16},{8,24},{16,0},{24,8},{1,17},{9,25},{17,1},{25,9},{2,18},{10... | collective-permute-start | bytes 1572872 | tf_op jit(solution)/shard_map/ppermute | solution.py:61
  263.8 24.7 %copy-start.14 = (f32[8,1024]{1,0:T(8,128)S(1)}, f32[8,1024]{1,0:T(8,128)}, u32[]{:S(2)}) copy-start(f32[8,1024]{1,0:T(8,128)} %param.9) | copy-start | bytes 98308
  263.9 14.1 %collective-permute-start.15 = (f32[16,64,128]{2,1,0:T(8,128)S(1)}, f32[16,64,128]{2,1,0:T(8,128)S(1)}, u32[]{:S(2)}, u32[]{:S(2)}) collective-permute-start(f32[16,64,128]{2,1,0:T(8,128)S(1)} %dynamic-slice_bitcast_fusion), channel_id=1, source_target_pairs={{0,8},{8,0},{16,24},{24,16},{1,9},{9,1},{17,25},{25,17},{2,10},{10... | collective-permute-start | bytes 1572872 | tf_op jit(solution)/shard_map/ppermute | solution.py:61
  284.0 30.8 %all-to-all-start.3 = ((f32[16,128,128]{2,1,0:T(8,128)}), f32[16,128,128]{2,1,0:T(8,128)}, u32[]{:S(2)}, u32[]{:S(2)}) async-start(f32[16,128,128]{2,1,0:T(8,128)} %pad_maximum_fusion.6), calls=%async_computation.3 | async-start | bytes 2097152 | tf_op jit(solution)/shard_map/all_to_all | solution.py:92
  335.1 7.8 %copy-start.12 = (f32[2,1024,128]{1,2,0:T(8,128)S(1)}, f32[2,1024,128]{1,2,0:T(8,128)}, u32[]{:S(2)}) copy-start(f32[2,1024,128]{1,2,0:T(8,128)} %all_to_all.67) | copy-start | bytes 3145732
where the time goes:
time: 366 us; the launch traced here: 359 us
  local copies, waits for them, and re-layouts  135 us (37%)
  matrix products  86.2 us (24%)
  waiting for transfers between devices  70.3 us (19%)
  starting transfers between devices  38.1 us (10%)
  other arithmetic  28.7 us (8%)
    unnamed x47, local copies, waits for them, and re-layouts  48.9 us
    ppermute x16, waiting for transfers between devices, reduce_over_bl(): parts[p] = keep + lax.ppermute(send, 'bl', perm=pairs)  46.5 us
    dot_general x4, matrix products, weigh_all(): jnp.einsum('mfg,mgk->mfk', inverse_cov, owner_modes, precision=lax.Precis...  31 us
    dynamic_slice x8, local copies, waits for them, and re-layouts, reduce_over_bl(): keep = lax.dynamic_index_in_dim(parts[p], mine, axis, keepdims=False)  29.7 us
    dot_general x1, matrix products, transform(): lax.dot_general(samples, dft_weights, (((0, 3), (0, 1)), ((), ())), prefe...  24 us
    all_to_all x4, waiting for transfers between devices, body(): lax.all_to_all(summed_modes, 'freq', split_axis=0, concat_axis=1, tiled=T...  23.8 us
    all_to_all x4, starting transfers between devices, body(): lax.all_to_all(summed_modes, 'freq', split_axis=0, concat_axis=1, tiled=T...  19.4 us
    ppermute x16, starting transfers between devices, reduce_over_bl(): parts[p] = keep + lax.ppermute(send, 'bl', perm=pairs)  18.7 us
  transfers between devices with their start and end apart: 20, of which 8 were waited for; matrix products, arithmetic and copies ran while one was open for 37% of the time, Pallas kernels for 0%

commit v1 on v0

--- a/solution.py
+++ b/solution.py
@@ -36,36 +36,31 @@
     dims = (((0,), (2,)), ((3,), (0,)))
     projected = lax.dot_general(high, beam_rows, dims, preferred_element_type=jnp.float32)
     projected = projected + lax.dot_general(low, beam_rows, dims, preferred_element_type=jnp.float32)
-    return projected.reshape(mode_count, freq_count, 2 * beam_rows.shape[1])
+    return projected
 
 
 def reduce_over_bl(partial, bl_devices):
     bits = bl_devices.bit_length() - 1
-    if bits == 0 or (1 << bits) != bl_devices or partial.shape[1] % 2:
-        return lax.psum_scatter(partial, "bl", scatter_dimension=0, tiled=True)
-    me = lax.axis_index("bl")
-    rows, freq_count = partial.shape[0], partial.shape[1]
+    rows = partial.shape[0]
     grid = partial.reshape((2,) * bits + (rows // bl_devices,) + partial.shape[1:])
-    half = freq_count // 2
-    parts = [grid[..., :half, :], grid[..., half:, :]]
+    parts = [grid[..., 0:1, :], grid[..., 1:2, :]]
     orders = [list(range(bits)), list(reversed(range(bits)))]
     axis_bits = [[bits - 1 - a for a in range(bits)] for _ in parts]
     for step in range(bits):
         for p in range(len(parts)):
             bit = orders[p][step]
             axis = axis_bits[p].index(bit)
-            mine = (me >> bit) & 1
-            keep = lax.dynamic_index_in_dim(parts[p], mine, axis, keepdims=False)
-            send = lax.dynamic_index_in_dim(parts[p], 1 - mine, axis, keepdims=False)
+            keep = lax.index_in_dim(parts[p], 0, axis, keepdims=False)
+            send = lax.index_in_dim(parts[p], 1, axis, keepdims=False)
             pairs = [(q, q ^ (1 << bit)) for q in range(bl_devices)]
             parts[p] = keep + lax.ppermute(send, "bl", perm=pairs)
             axis_bits[p].pop(axis)
-    return jnp.concatenate(parts, axis=1)
+    return jnp.concatenate(parts, axis=2)
 
 
 def weigh_all(inverse_cov, noise_power, owner_modes):
-    weighted = jnp.einsum("mfg,mgk->mfk", inverse_cov, owner_modes, precision=lax.Precision.HIGH)
-    return owner_modes - noise_power[:, :, None] * weighted
+    weighted = jnp.einsum("mfg,mgcs->mfcs", inverse_cov, owner_modes, precision=lax.Precision.HIGH)
+    return owner_modes - noise_power[:, :, None, None] * weighted
 
 
 def body(visibility, mode_index, beam_mode_weights, inverse_cov, noise_power):
@@ -76,11 +71,15 @@
     owned = inverse_cov.shape[0]
     chunk_count = math.gcd(CHUNKS, owned)
     chunk = owned // chunk_count
-    sample_ids = lax.axis_index("bl") * local_times + jnp.arange(local_times, dtype=jnp.int32)
-    index_grid = mode_index.reshape(bl_devices, freq_devices, chunk_count, chunk)
+    me = lax.axis_index("bl")
+    sample_ids = me * local_times + jnp.arange(local_times, dtype=jnp.int32)
+    owners = jnp.bitwise_xor(me, jnp.arange(bl_devices, dtype=jnp.int32))
+    index_grid = jnp.take(mode_index.reshape(bl_devices, freq_devices, chunk_count, chunk), owners, axis=0)
     ordered_modes = jnp.transpose(index_grid, (2, 0, 1, 3)).reshape(-1)
     beam_tail = beam_mode_weights.shape[1:]
-    beam_grid = beam_mode_weights.reshape((bl_devices, freq_devices, chunk_count, chunk) + beam_tail)
+    beam_grid = jnp.take(
+        beam_mode_weights.reshape((bl_devices, freq_devices, chunk_count, chunk) + beam_tail), owners, axis=0
+    )
     dft_weights = dft_table(ordered_modes, sample_ids, total_times, chunk_count)
     spectrum = transform(visibility, dft_weights)
     width = spectrum.shape[2] // chunk_count
@@ -89,12 +88,15 @@
         beams = beam_grid[:, :, step].reshape((-1,) + beam_tail)
         partial_terms = project(spectrum[:, :, step * width:(step + 1) * width], beams)
         summed_modes = reduce_over_bl(partial_terms, bl_devices)
+        if pieces:
+            summed_modes, pieces[-1] = lax.optimization_barrier((summed_modes, pieces[-1]))
         owner_modes = lax.all_to_all(summed_modes, "freq", split_axis=0, concat_axis=1, tiled=True)
         lo = step * chunk
         pieces.append(
             weigh_all(inverse_cov[lo:lo + chunk], noise_power[lo:lo + chunk], owner_modes)
         )
-    return jnp.concatenate(pieces, axis=0)
+    filtered = jnp.concatenate(pieces, axis=0)
+    return filtered.reshape(filtered.shape[:2] + (-1,))
 
 
 def solution(mesh):

time: 366 us -> 336 us (0.918)
  local copies, waits for them, and re-layouts: 135 us -> 44.5 us
  waiting for transfers between devices: 70.3 us -> 113 us
  blocking collectives: 0 us -> 29.3 us
  other arithmetic: 28.7 us -> 21 us
    ppermute x16, waiting for transfers between devices: 46.5 us -> 96.8 us  [reduce_over_bl(): parts[p] = keep + lax.ppermute(send, 'bl', perm=pairs)]
    unnamed x47 -> x25, local copies, waits for them, and re-layouts: 48.9 us -> 8.36 us
    dynamic_slice x8 -> x0, local copies, waits for them, and re-layouts: 29.7 us -> none  [reduce_over_bl(): keep = lax.dynamic_index_in_dim(parts[p], mine, axis, keepdims=False)]
    all_to_all x0 -> x1, blocking collectives: none -> 29.3 us  [body(): lax.all_to_all(summed_modes, 'freq', split_axis=0, concat_axis=1, tiled=T...]
    slice x4 -> x0, local copies, waits for them, and re-layouts: 17.4 us -> none  [reduce_over_bl(): parts = [grid[..., :half, :], grid[..., half:, :]]]
    all_to_all x8 -> x4, local copies, waits for them, and re-layouts: 12.4 us -> 1.54 us  [body(): lax.all_to_all(summed_modes, 'freq', split_axis=0, concat_axis=1, tiled=T...]
    add x16 -> x12, other arithmetic: 17.2 us -> 7.76 us  [reduce_over_bl(): parts[p] = keep + lax.ppermute(send, 'bl', perm=pairs)]
    all_to_all x4 -> x3, waiting for transfers between devices: 23.8 us -> 16.6 us  [body(): lax.all_to_all(summed_modes, 'freq', split_axis=0, concat_axis=1, tiled=T...]
  transfers between devices with their start and end apart: 20 -> 19, of which waited for: 8 -> 13; matrix products, arithmetic and copies ran while one was open for 37% -> 19% of each run, Pallas kernels for 0% -> 0%
where the time goes in v1:
time: 336 us; the launch traced here: 330 us
  waiting for transfers between devices  113 us (34%)
  matrix products  85.1 us (25%)
  local copies, waits for them, and re-layouts  44.5 us (13%)
  starting transfers between devices  35.2 us (10%)
  blocking collectives  29.3 us (9%)
  other arithmetic  21 us (6%)
    ppermute x16, waiting for transfers between devices, reduce_over_bl(): parts[p] = keep + lax.ppermute(send, 'bl', perm=pairs)  96.8 us
    dot_general x4, matrix products, weigh_all(): jnp.einsum('mfg,mgcs->mfcs', inverse_cov, owner_modes, precision=lax.Prec...  31.7 us
    all_to_all x1, blocking collectives, body(): lax.all_to_all(summed_modes, 'freq', split_axis=0, concat_axis=1, tiled=T...  29.3 us
    dot_general x1, matrix products, transform(): lax.dot_general(samples, dft_weights, (((0, 3), (0, 1)), ((), ())), prefe...  24 us
    ppermute x16, starting transfers between devices, reduce_over_bl(): parts[p] = keep + lax.ppermute(send, 'bl', perm=pairs)  21.5 us
    all_to_all x3, waiting for transfers between devices, body(): lax.all_to_all(summed_modes, 'freq', split_axis=0, concat_axis=1, tiled=T...  16.6 us
    dot_general x4, matrix products, project(): lax.dot_general(low, beam_rows, dims, preferred_element_type=jnp.float32)  16.3 us
    all_to_all x3, starting transfers between devices, body(): lax.all_to_all(summed_modes, 'freq', split_axis=0, concat_axis=1, tiled=T...  13.7 us
  transfers between devices with their start and end apart: 19, of which 13 were waited for; matrix products, arithmetic and copies ran while one was open for 19% of the time, Pallas kernels for 0%

profile of v1, /device:TPU:0, one launch (start us, length us, event | category | flops | bytes accessed | tf_op | source)
XLA Modules:
  0.0 329.6 jit_solution(15419693445277205172)
XLA Ops:
  0.0 0.8 reshape.166
  1.9 4.6 %negate_convert_fusion = (bf16[1024,4,1,64]{0,3,2,1:T(8,128)(2,1)S(1)}, bf16[1024,4,1,64]{0,3,2,1:T(8,128)(2,1)S(1)}, bf16[1024,4,1,64]{0,3,2,1:T(8,128)(2,1)S(1)}) fusion(s32[1024]{0:T(1024)S(1)} %iota_add_fusion, s32[4,64]{1,0:T(4,128)S(1)} %copy.74), kind=kLoop, calls=%fused_computation.97 | loop fusion | flops 5242880 | bytes 1577984 | tf_op jit(solution)/shard_map/convert.7
  6.7 24.0 %convolution_bitcast_fusion = f32[64,128,512]{1,2,0:T(8,128)} fusion(bf16[2,64,128,1024]{3,2,1,0:T(8,128)(2,1)} %param.5, bf16[1,1024,512]{1,2,0:T(8,128)(2,1)S(1)} %bitcast.331, bf16[1,1024,512]{1,2,0:T(8,128)(2,1)S(1)} %bitcast.330), kind=kOutput, calls=%fused_computation.2 | convolution fusion | flops 17184063488 | bytes 52428800 | tf_op jit(solution)/shard_map/dot_general | solution.py:24
  30.7 12.5 %fusion.90 = (f32[64,128,128]{1,2,0:T(8,128)}, f32[64,128,128]{1,2,0:T(8,128)}, f32[64,128,128]{1,2,0:T(8,128)}, f32[64,128,128]{1,2,0:T(8,128)}) fusion(f32[64,128,512]{1,2,0:T(8,128)} %convolution_bitcast_fusion), kind=kLoop, calls=%fused_computation.133 | loop fusion | bytes 33554432 | tf_op jit(solution)/shard_map/slice | solution.py:89
  43.1 7.1 %copy.77 = bf16[256,64,64]{2,1,0:T(8,128)(2,1)} copy(bf16[256,64,64]{0,2,1:T(8,128)(2,1)S(1)} %copy-done.7) | data formatting | bytes 4194304 | tf_op args[2]
  50.3 5.4 %gather_fusion.1 = bf16[4,8,4,2,64,64]{5,4,3,2,1,0:T(8,128)(2,1)} fusion(bf16[4,8,4,2,64,64]{5,4,3,2,1,0:T(8,128)(2,1)} %bitcast.315, s32[1024]{0:T(1024)} %copy-done.9), kind=kCustom, calls=%fused_computation.1 | custom fusion | bytes 4194320 | tf_op jit(solution)/shard_map/jit(_take)/gather | solution.py:80
  55.7 2.7 broadcast_select_fusion
  58.3 1.0 fusion.91
  59.3 1.2 copy-done.3
  60.5 2.8 fusion.21
  63.3 2.7 convolution_add_fusion.2
  66.1 3.0 collective-permute-start.4
  69.2 1.6 collective-permute-start.6
  70.8 2.8 fusion.20
  73.6 2.8 convolution_add_fusion.3
  77.2 1.4 collective-permute-start.2
  78.6 2.8 fusion.22
  81.4 2.7 convolution_add_fusion.1
  84.1 1.1 slice_bitcast_fusion.4
  85.2 0.7 collective-permute-start.10
  85.9 4.8 %fusion.23 = f32[64,128,2,64]{1,3,2,0:T(8,128)} fusion(bf16[64,64,64,1]{2,1,3,0:T(8,128)(2,1)S(1)} %bitcast.316, f32[64,128,2,64]{1,3,2,0:T(8,128)S(1)} %bitcast.295), kind=kOutput, calls=%fused_computation.36 | convolution fusion | flops 136314880 | bytes 8912896 | tf_op jit(solution)/shard_map/dot_general | solution.py:37
  90.7 1.0 slice_bitcast_fusion.6
  91.7 1.3 collective-permute-done.4
  93.1 2.1 collective-permute-start.8
  95.9 1.6 collective-permute-start.5
  97.6 18.0 %collective-permute-done = f32[2,16,128,1,64]{2,4,1,3,0:T(8,128)S(1)} collective-permute-done((f32[2,16,128,1,64]{2,4,1,3,0:T(8,128)S(1)}, f32[2,16,128,1,64]{2,4,1,3,0:T(8,128)S(1)}, u32[]{:S(2)}, u32[]{:S(2)}) %collective-permute-start) | collective-permute-done | bytes 1048608 | tf_op jit(solution)/shard_map/ppermute | solution.py:56
  115.5 2.1 collective-permute-start.7
  117.8 1.6 fusion.78
  119.4 30.7 %collective-permute-done.5 = f32[16,128,1,64]{1,3,2,0:T(8,128)S(1)} collective-permute-done((f32[16,128,1,64]{1,3,2,0:T(8,128)S(1)}, f32[16,128,1,64]{1,3,2,0:T(8,128)S(1)}, u32[]{:S(2)}, u32[]{:S(2)}) %collective-permute-start.5) | collective-permute-done | bytes 524320 | tf_op jit(solution)/shard_map/ppermute | solution.py:56
  150.2 1.1 pad_maximum_fusion.4
  151.3 5.1 %all-to-all-start = ((f32[16,128,2,64]{1,3,2,0:T(8,128)}), f32[16,128,2,64]{1,3,2,0:T(8,128)S(1)}, u32[]{:S(2)}, u32[]{:S(2)}) async-start(f32[16,128,2,64]{1,3,2,0:T(8,128)} %pad_maximum_fusion.4), calls=%async_computation | async-start | bytes 2097152 | tf_op jit(solution)/shard_map/all_to_all | solution.py:93
  156.4 1.1 slice_bitcast_fusion.30
  157.5 1.6 collective-permute-start.1
  159.1 0.6 collective-permute-start.3
  159.7 8.2 %convolution_add_fusion = f32[64,128,2,64]{1,3,2,0:T(8,128)} fusion(f32[64,128,2,64]{1,3,2,0:T(8,128)} %fusion.23, bf16[64,64,64,1]{2,1,3,0:T(8,128)(2,1)S(1)} %bitcast.317, f32[64,128,2,64]{1,3,2,0:T(8,128)} %bitcast.294), kind=kOutput, calls=%fused_computation.29 | convolution fusion | flops 138412032 | bytes 13107200 | tf_op jit(solution)/shard_map/dot_general | solution.py:38
  167.9 4.0 %collective-permute-done.1 = f32[16,128,1,64]{1,3,2,0:T(8,128)S(1)} collective-permute-done((f32[16,128,1,64]{1,3,2,0:T(8,128)S(1)}, f32[16,128,1,64]{1,3,2,0:T(8,128)S(1)}, u32[]{:S(2)}, u32[]{:S(2)}) %collective-permute-start.1) | collective-permute-done | bytes 524320 | tf_op jit(solution)/shard_map/ppermute | solution.py:56
  171.9 1.3 collective-permute-done.3
  173.3 1.1 pad_maximum_fusion.3
  174.4 8.5 %all-to-all-done = f32[16,128,2,64]{1,3,2,0:T(8,128)S(1)} async-done(((f32[16,128,2,64]{1,3,2,0:T(8,128)}), f32[16,128,2,64]{1,3,2,0:T(8,128)S(1)}, u32[]{:S(2)}, u32[]{:S(2)}) %all-to-all-start) | async-done | bytes 1048608 | tf_op jit(solution)/shard_map/all_to_all | solution.py:93
  182.9 0.6 copy.168
  183.7 7.6 %fusion.34 = f32[2,1024,2,64]{1,3,2,0:T(8,128)S(1)} fusion(f32[2,1024,2,64]{1,3,2,0:T(8,128)S(1)} %all_to_all.55, f32[8,1024,1024]{2,1,0:T(8,128)} %param.8, f32[2,1024]{1,0:T(2,128)S(1)} %get-tuple-element.37), kind=kOutput, calls=%fused_computation.48 | convolution fusion | flops 1611137024 | bytes 11542528 | tf_op jit(solution)/shard_map/mfg,mgcs->mfcs/dot_general | solution.py:62
  191.4 3.8 %all-to-all-start.1 = ((f32[16,128,2,64]{1,3,2,0:T(8,128)}), f32[16,128,2,64]{1,3,2,0:T(8,128)S(1)}, u32[]{:S(2)}, u32[]{:S(2)}) async-start(f32[16,128,2,64]{1,3,2,0:T(8,128)} %pad_maximum_fusion.3), calls=%async_computation.1 | async-start | bytes 2097152 | tf_op jit(solution)/shard_map/all_to_all | solution.py:93
  195.2 2.4 slice_bitcast_fusion.2
  198.2 2.6 fusion.74
  200.8 1.6 collective-permute-start.9
  202.4 1.6 collective-permute-start.11
  204.0 2.3 slice_bitcast_fusion
  206.8 8.8 %collective-permute-done.9 = f32[16,128,1,64]{1,3,2,0:T(8,128)S(1)} collective-permute-done((f32[16,128,1,64]{1,3,2,0:T(8,128)S(1)}, f32[16,128,1,64]{1,3,2,0:T(8,128)S(1)}, u32[]{:S(2)}, u32[]{:S(2)}) %collective-permute-start.9) | collective-permute-done | bytes 524320 | tf_op jit(solution)/shard_map/ppermute | solution.py:56
  215.7 18.9 %collective-permute-done.11 = f32[16,128,1,64]{1,3,2,0:T(8,128)S(1)} collective-permute-done((f32[16,128,1,64]{1,3,2,0:T(8,128)S(1)}, f32[16,128,1,64]{1,3,2,0:T(8,128)S(1)}, u32[]{:S(2)}, u32[]{:S(2)}) %collective-permute-start.11) | collective-permute-done | bytes 524320 | tf_op jit(solution)/shard_map/ppermute | solution.py:56
  234.7 1.1 pad_maximum_fusion.5
  235.7 0.6 copy.167
  236.5 8.6 %fusion.43 = f32[2,1024,2,64]{1,3,2,0:T(8,128)} fusion(f32[2,1024,2,64]{1,3,2,0:T(8,128)S(1)} %all_to_all.59, f32[8,1024,1024]{2,1,0:T(8,128)} %param.8, f32[2,1024]{1,0:T(2,128)S(1)} %get-tuple-element.36), kind=kOutput, calls=%fused_computation.51 | convolution fusion | flops 1611137024 | bytes 11542528 | tf_op jit(solution)/shard_map/mfg,mgcs->mfcs/dot_general | solution.py:62
  245.1 4.8 %all-to-all-start.2 = ((f32[16,128,2,64]{1,3,2,0:T(8,128)}), f32[16,128,2,64]{1,3,2,0:T(8,128)S(1)}, u32[]{:S(2)}, u32[]{:S(2)}) async-start(f32[16,128,2,64]{1,3,2,0:T(8,128)} %pad_maximum_fusion.5), calls=%async_computation.2 | async-start | bytes 2097152 | tf_op jit(solution)/shard_map/all_to_all | solution.py:93
  249.9 2.6 fusion.72
  252.5 1.6 collective-permute-start.13
  254.1 0.6 collective-permute-start.15
  254.7 12.2 %collective-permute-done.13 = f32[16,128,1,64]{1,3,2,0:T(8,128)S(1)} collective-permute-done((f32[16,128,1,64]{1,3,2,0:T(8,128)S(1)}, f32[16,128,1,64]{1,3,2,0:T(8,128)S(1)}, u32[]{:S(2)}, u32[]{:S(2)}) %collective-permute-start.13) | collective-permute-done | bytes 524320 | tf_op jit(solution)/shard_map/ppermute | solution.py:56
  267.0 1.3 collective-permute-done.15
  268.4 8.1 %all-to-all-done.2 = f32[16,128,2,64]{1,3,2,0:T(8,128)S(1)} async-done(((f32[16,128,2,64]{1,3,2,0:T(8,128)}), f32[16,128,2,64]{1,3,2,0:T(8,128)S(1)}, u32[]{:S(2)}, u32[]{:S(2)}) %all-to-all-start.2) | async-done | bytes 1048608 | tf_op jit(solution)/shard_map/all_to_all | solution.py:93
  276.5 7.6 %fusion.52 = f32[2,1024,2,64]{1,3,2,0:T(8,128)S(1)} fusion(f32[8,1024,1024]{2,1,0:T(8,128)} %param.8, f32[8,2,2,8,8,128]{5,4,3,2,1,0:T(8,128)S(1)} %bitcast.324, f32[2,1024]{1,0:T(2,128)S(1)} %get-tuple-element.38), kind=kOutput, calls=%fused_computation.54 | convolution fusion | flops 1611137024 | bytes 11542528 | tf_op jit(solution)/shard_map/mfg,mgcs->mfcs/dot_general | solution.py:62
  284.1 29.3 %all_to_all.72 = f32[16,128,2,64]{1,3,2,0:T(8,128)S(1)} all-to-all(f32[16,128,2,64]{1,3,2,0:T(8,128)S(1)} %pad_maximum_fusion.6), channel_id=1, replica_groups=mesh['bl'=4,'freq'=8] {'freq'}, dimensions={0} | all-to-all | bytes 2097152 | tf_op jit(solution)/shard_map/all_to_all | solution.py:93
  313.4 7.8 %fusion.61 = f32[2,1024,2,64]{1,3,2,0:T(8,128)S(1)} fusion(f32[8,1024,1024]{2,1,0:T(8,128)} %param.8, f32[8,2,2,8,8,128]{5,4,3,2,1,0:T(8,128)S(1)} %bitcast.325, f32[2,1024]{1,0:T(2,128)S(1)} %get-tuple-element.35), kind=kOutput, calls=%fused_computation.57 | convolution fusion | flops 1611137024 | bytes 11542528 | tf_op jit(solution)/shard_map/mfg,mgcs->mfcs/dot_general | solution.py:62
  321.2 2.5 pad_maximum_fusion
  323.7 5.3 %copy.113 = f32[8,1024,128]{2,1,0:T(8,128)} copy(f32[8,1024,128]{1,2,0:T(8,128)} %bitcast.314) | data formatting | bytes 8388608 | tf_op jit(solution)/shard_map/reshape | solution.py:99
  (68 shorter events, 5.5 us)
Async XLA Ops:
  0.0 6.7 %copy-start.10 = (pred[4]{0:T(512)(128)(4,1)}, pred[4]{0:T(512)(128)(4,1)S(1)}, u32[]{:S(2)}) copy-start(pred[4]{0:T(512)(128)(4,1)S(1)} %compare_and_fusion) | copy-start | bytes 16
  0.0 6.7 %copy-start.9 = (s32[1024]{0:T(1024)}, s32[1024]{0:T(1024)S(1)}, u32[]{:S(2)}) copy-start(s32[1024]{0:T(1024)S(1)} %pad_clamp_fusion) | copy-start | bytes 12292
  30.7 12.5 %copy-start.7 = (bf16[256,64,64]{0,2,1:T(8,128)(2,1)S(1)}, bf16[256,64,64]{0,2,1:T(8,128)(2,1)}, u32[]{:S(2)}) copy-start(bf16[256,64,64]{0,2,1:T(8,128)(2,1)} %param.7) | copy-start | bytes 6291460
  50.3 5.4 %copy-start.11 = (pred[4]{0:T(512)(128)(4,1)S(1)}, pred[4]{0:T(512)(128)(4,1)}, u32[]{:S(2)}) copy-start(pred[4]{0:T(512)(128)(4,1)} %copy-done.10) | copy-start | bytes 16
  58.3 2.2 copy-start.3
  65.9 4.8 %copy-start.2 = (f32[64,128,128]{1,2,0:T(8,128)S(1)}, f32[64,128,128]{1,2,0:T(8,128)}, u32[]{:S(2)}) copy-start(f32[64,128,128]{1,2,0:T(8,128)} %get-tuple-element.20) | copy-start | bytes 12582916
  66.1 27.0 %collective-permute-start.4 = (f32[2,16,128,1,64]{2,4,1,3,0:T(8,128)S(1)}, f32[2,16,128,1,64]{2,4,1,3,0:T(8,128)S(1)}, u32[]{:S(2)}, u32[]{:S(2)}) collective-permute-start(f32[2,16,128,1,64]{2,4,1,3,0:T(8,128)S(1)} %slice_bitcast_fusion.10), channel_id=1, source_target_pairs={{0,8},{8,0},{16,24},{24,16},{1,9},{9,1},{17,25},{25,17},{2,10},{10... | collective-permute-start | bytes 3145736 | tf_op jit(solution)/shard_map/ppermute | solution.py:56
  69.2 26.2 %collective-permute-start.6 = (f32[2,16,128,1,64]{2,4,1,3,0:T(8,128)S(1)}, f32[2,16,128,1,64]{2,4,1,3,0:T(8,128)S(1)}, u32[]{:S(2)}, u32[]{:S(2)}) collective-permute-start(f32[2,16,128,1,64]{2,4,1,3,0:T(8,128)S(1)} %slice_bitcast_fusion.8), channel_id=1, source_target_pairs={{0,16},{8,24},{16,0},{24,8},{1,17},{9,25},{17,1},{25,9},{2,18},{10... | collective-permute-start | bytes 3145736 | tf_op jit(solution)/shard_map/ppermute | solution.py:56
  76.4 2.2 copy-start.1
  76.5 39.0 %collective-permute-start = (f32[2,16,128,1,64]{2,4,1,3,0:T(8,128)S(1)}, f32[2,16,128,1,64]{2,4,1,3,0:T(8,128)S(1)}, u32[]{:S(2)}, u32[]{:S(2)}) collective-permute-start(f32[2,16,128,1,64]{2,4,1,3,0:T(8,128)S(1)} %slice_bitcast_fusion.14), channel_id=1, source_target_pairs={{0,8},{8,0},{16,24},{24,16},{1,9},{9,1},{17,25},{25,17},{2,10},{10... | collective-permute-start | bytes 3145736 | tf_op jit(solution)/shard_map/ppermute | solution.py:56
  77.2 40.6 %collective-permute-start.2 = (f32[2,16,128,1,64]{2,4,1,3,0:T(8,128)S(1)}, f32[2,16,128,1,64]{2,4,1,3,0:T(8,128)S(1)}, u32[]{:S(2)}, u32[]{:S(2)}) collective-permute-start(f32[2,16,128,1,64]{2,4,1,3,0:T(8,128)S(1)} %slice_bitcast_fusion.12), channel_id=1, source_target_pairs={{0,16},{8,24},{16,0},{24,8},{1,17},{9,25},{17,1},{25,9},{2,18},{10... | collective-permute-start | bytes 3145736 | tf_op jit(solution)/shard_map/ppermute | solution.py:56
  81.4 4.5 %copy-start = (f32[64,128,128]{1,2,0:T(8,128)S(1)}, f32[64,128,128]{1,2,0:T(8,128)}, u32[]{:S(2)}) copy-start(f32[64,128,128]{1,2,0:T(8,128)} %get-tuple-element.18) | copy-start | bytes 12582916
  84.0 6.7 %copy-start.4 = (f32[64,128,2,64]{1,3,2,0:T(8,128)}, f32[64,128,2,64]{1,3,2,0:T(8,128)S(1)}, u32[]{:S(2)}) copy-start(f32[64,128,2,64]{1,3,2,0:T(8,128)S(1)} %convolution_add_fusion.1) | copy-start | bytes 12582916
  85.2 113.0 %collective-permute-start.10 = (f32[2,16,128,1,64]{2,4,1,3,0:T(8,128)}, f32[2,16,128,1,64]{2,4,1,3,0:T(8,128)}, u32[]{:S(2)}, u32[]{:S(2)}) collective-permute-start(f32[2,16,128,1,64]{2,4,1,3,0:T(8,128)} %slice_bitcast_fusion.4), channel_id=1, source_target_pairs={{0,16},{8,24},{16,0},{24,8},{1,17},{9,25},{17,1},{25,9},{2,18},{10... | collective-permute-start | bytes 3145736 | tf_op jit(solution)/shard_map/ppermute | solution.py:56
  93.1 105.1 %collective-permute-start.8 = (f32[2,16,128,1,64]{2,4,1,3,0:T(8,128)}, f32[2,16,128,1,64]{2,4,1,3,0:T(8,128)}, u32[]{:S(2)}, u32[]{:S(2)}) collective-permute-start(f32[2,16,128,1,64]{2,4,1,3,0:T(8,128)} %slice_bitcast_fusion.6), channel_id=1, source_target_pairs={{0,8},{8,0},{16,24},{24,16},{1,9},{9,1},{17,25},{25,17},{2,10},{10... | collective-permute-start | bytes 3145736 | tf_op jit(solution)/shard_map/ppermute | solution.py:56
  95.9 54.1 %collective-permute-start.5 = (f32[16,128,1,64]{1,3,2,0:T(8,128)S(1)}, f32[16,128,1,64]{1,3,2,0:T(8,128)S(1)}, u32[]{:S(2)}, u32[]{:S(2)}) collective-permute-start(f32[16,128,1,64]{1,3,2,0:T(8,128)S(1)} %slice_bitcast_fusion.26), channel_id=1, source_target_pairs={{0,16},{8,24},{16,0},{24,8},{1,17},{9,25},{17,1},{25,9},{2,18},{10... | collective-permute-start | bytes 1572872 | tf_op jit(solution)/shard_map/ppermute | solution.py:56
  115.5 34.6 %collective-permute-start.7 = (f32[16,128,1,64]{1,3,2,0:T(8,128)S(1)}, f32[16,128,1,64]{1,3,2,0:T(8,128)S(1)}, u32[]{:S(2)}, u32[]{:S(2)}) collective-permute-start(f32[16,128,1,64]{1,3,2,0:T(8,128)S(1)} %slice_bitcast_fusion.24), channel_id=1, source_target_pairs={{0,8},{8,0},{16,24},{24,16},{1,9},{9,1},{17,25},{25,17},{2,10},{10... | collective-permute-start | bytes 1572872 | tf_op jit(solution)/shard_map/ppermute | solution.py:56
  151.3 31.7 %all-to-all-start = ((f32[16,128,2,64]{1,3,2,0:T(8,128)}), f32[16,128,2,64]{1,3,2,0:T(8,128)S(1)}, u32[]{:S(2)}, u32[]{:S(2)}) async-start(f32[16,128,2,64]{1,3,2,0:T(8,128)} %pad_maximum_fusion.4), calls=%async_computation | async-start | bytes 2097152 | tf_op jit(solution)/shard_map/all_to_all | solution.py:93
  157.5 14.4 %collective-permute-start.1 = (f32[16,128,1,64]{1,3,2,0:T(8,128)S(1)}, f32[16,128,1,64]{1,3,2,0:T(8,128)S(1)}, u32[]{:S(2)}, u32[]{:S(2)}) collective-permute-start(f32[16,128,1,64]{1,3,2,0:T(8,128)S(1)} %slice_bitcast_fusion.30), channel_id=1, source_target_pairs={{0,16},{8,24},{16,0},{24,8},{1,17},{9,25},{17,1},{25,9},{2,18},{10... | collective-permute-start | bytes 1572872 | tf_op jit(solution)/shard_map/ppermute | solution.py:56
  159.1 8.8 %copy-start.8 = (f32[8,1024]{1,0:T(8,128)S(1)}, f32[8,1024]{1,0:T(8,128)}, u32[]{:S(2)}) copy-start(f32[8,1024]{1,0:T(8,128)} %param.9) | copy-start | bytes 98308
  159.1 12.8 %copy-start.5 = (f32[2,16,128,1,64]{2,4,1,3,0:T(8,128)S(1)}, f32[2,16,128,1,64]{2,4,1,3,0:T(8,128)}, u32[]{:S(2)}) copy-start(f32[2,16,128,1,64]{2,4,1,3,0:T(8,128)} %get-tuple-element.27) | copy-start | bytes 3145732
  159.1 14.1 %collective-permute-start.3 = (f32[16,128,1,64]{1,3,2,0:T(8,128)S(1)}, f32[16,128,1,64]{1,3,2,0:T(8,128)S(1)}, u32[]{:S(2)}, u32[]{:S(2)}) collective-permute-start(f32[16,128,1,64]{1,3,2,0:T(8,128)S(1)} %slice_bitcast_fusion.28), channel_id=1, source_target_pairs={{0,8},{8,0},{16,24},{24,16},{1,9},{9,1},{17,25},{25,17},{2,10},{10... | collective-permute-start | bytes 1572872 | tf_op jit(solution)/shard_map/ppermute | solution.py:56
  191.4 44.3 %all-to-all-start.1 = ((f32[16,128,2,64]{1,3,2,0:T(8,128)}), f32[16,128,2,64]{1,3,2,0:T(8,128)S(1)}, u32[]{:S(2)}, u32[]{:S(2)}) async-start(f32[16,128,2,64]{1,3,2,0:T(8,128)} %pad_maximum_fusion.3), calls=%async_computation.1 | async-start | bytes 2097152 | tf_op jit(solution)/shard_map/all_to_all | solution.py:93
  197.6 52.3 %collective-permute-start.12 = (f32[2,16,128,1,64]{2,4,1,3,0:T(8,128)}, f32[2,16,128,1,64]{2,4,1,3,0:T(8,128)}, u32[]{:S(2)}, u32[]{:S(2)}) collective-permute-start(f32[2,16,128,1,64]{2,4,1,3,0:T(8,128)} %slice_bitcast_fusion.2), channel_id=1, source_target_pairs={{0,8},{8,0},{16,24},{24,16},{1,9},{9,1},{17,25},{25,17},{2,10},{10... | collective-permute-start | bytes 3145736 | tf_op jit(solution)/shard_map/ppermute | solution.py:56
  200.8 14.8 %collective-permute-start.9 = (f32[16,128,1,64]{1,3,2,0:T(8,128)S(1)}, f32[16,128,1,64]{1,3,2,0:T(8,128)S(1)}, u32[]{:S(2)}, u32[]{:S(2)}) collective-permute-start(f32[16,128,1,64]{1,3,2,0:T(8,128)S(1)} %slice_bitcast_fusion.22), channel_id=1, source_target_pairs={{0,16},{8,24},{16,0},{24,8},{1,17},{9,25},{17,1},{25,9},{2,18},{10... | collective-permute-start | bytes 1572872 | tf_op jit(solution)/shard_map/ppermute | solution.py:56
  202.4 32.2 %collective-permute-start.11 = (f32[16,128,1,64]{1,3,2,0:T(8,128)S(1)}, f32[16,128,1,64]{1,3,2,0:T(8,128)S(1)}, u32[]{:S(2)}, u32[]{:S(2)}) collective-permute-start(f32[16,128,1,64]{1,3,2,0:T(8,128)S(1)} %slice_bitcast_fusion.20), channel_id=1, source_target_pairs={{0,8},{8,0},{16,24},{24,16},{1,9},{9,1},{17,25},{25,17},{2,10},{10... | collective-permute-start | bytes 1572872 | tf_op jit(solution)/shard_map/ppermute | solution.py:56
  206.3 43.6 %collective-permute-start.14 = (f32[2,16,128,1,64]{2,4,1,3,0:T(8,128)}, f32[2,16,128,1,64]{2,4,1,3,0:T(8,128)}, u32[]{:S(2)}, u32[]{:S(2)}) collective-permute-start(f32[2,16,128,1,64]{2,4,1,3,0:T(8,128)} %slice_bitcast_fusion), channel_id=1, source_target_pairs={{0,16},{8,24},{16,0},{24,8},{1,17},{9,25},{17,1},{25,9},{2,18},{10... | collective-permute-start | bytes 3145736 | tf_op jit(solution)/shard_map/ppermute | solution.py:56
  245.1 31.4 %all-to-all-start.2 = ((f32[16,128,2,64]{1,3,2,0:T(8,128)}), f32[16,128,2,64]{1,3,2,0:T(8,128)S(1)}, u32[]{:S(2)}, u32[]{:S(2)}) async-start(f32[16,128,2,64]{1,3,2,0:T(8,128)} %pad_maximum_fusion.5), calls=%async_computation.2 | async-start | bytes 2097152 | tf_op jit(solution)/shard_map/all_to_all | solution.py:93
  252.5 14.4 %collective-permute-start.13 = (f32[16,128,1,64]{1,3,2,0:T(8,128)S(1)}, f32[16,128,1,64]{1,3,2,0:T(8,128)S(1)}, u32[]{:S(2)}, u32[]{:S(2)}) collective-permute-start(f32[16,128,1,64]{1,3,2,0:T(8,128)S(1)} %slice_bitcast_fusion.18), channel_id=1, source_target_pairs={{0,16},{8,24},{16,0},{24,8},{1,17},{9,25},{17,1},{25,9},{2,18},{10... | collective-permute-start | bytes 1572872 | tf_op jit(solution)/shard_map/ppermute | solution.py:56
  254.1 14.1 %collective-permute-start.15 = (f32[16,128,1,64]{1,3,2,0:T(8,128)S(1)}, f32[16,128,1,64]{1,3,2,0:T(8,128)S(1)}, u32[]{:S(2)}, u32[]{:S(2)}) collective-permute-start(f32[16,128,1,64]{1,3,2,0:T(8,128)S(1)} %slice_bitcast_fusion.16), channel_id=1, source_target_pairs={{0,8},{8,0},{16,24},{24,16},{1,9},{9,1},{17,25},{25,17},{2,10},{10... | collective-permute-start | bytes 1572872 | tf_op jit(solution)/shard_map/ppermute | solution.py:56
  313.4 7.8 %copy-start.6 = (f32[2,1024,2,64]{1,3,2,0:T(8,128)S(1)}, f32[2,1024,2,64]{1,3,2,0:T(8,128)}, u32[]{:S(2)}) copy-start(f32[2,1024,2,64]{1,3,2,0:T(8,128)} %fusion.43) | copy-start | bytes 3145732

commit v2 on v1

--- a/solution.py
+++ b/solution.py
@@ -39,6 +39,32 @@
     return projected
 
 
+RESIDUAL_LEVELS = 7
+RESIDUAL_SCALE = RESIDUAL_LEVELS * 256.0
+
+
+def encode_pairs(block, axis):
+    high = lax.reduce_precision(block, exponent_bits=8, mantissa_bits=7)
+    size = jnp.abs(high)
+    ratio = jnp.where(size > 0, (block - high) / jnp.where(size > 0, size, 1.0), 0.0)
+    steps = jnp.clip(jnp.round(ratio * RESIDUAL_SCALE), -RESIDUAL_LEVELS, RESIDUAL_LEVELS)
+    rows = block.shape[axis] // 2
+    first = lax.slice_in_dim(steps, 0, rows, axis=axis)
+    second = lax.slice_in_dim(steps, rows, 2 * rows, axis=axis)
+    code = first * (2 * RESIDUAL_LEVELS + 1) + second
+    return jnp.concatenate([high, code], axis=axis).astype(jnp.bfloat16)
+
+
+def decode_pairs(payload, axis):
+    rows = payload.shape[axis] // 3
+    high = lax.slice_in_dim(payload, 0, 2 * rows, axis=axis).astype(jnp.float32)
+    code = lax.slice_in_dim(payload, 2 * rows, 3 * rows, axis=axis).astype(jnp.float32)
+    first = jnp.round(code / (2 * RESIDUAL_LEVELS + 1))
+    second = code - first * (2 * RESIDUAL_LEVELS + 1)
+    steps = jnp.concatenate([first, second], axis=axis)
+    return high + jnp.abs(high) * (steps / RESIDUAL_SCALE)
+
+
 def reduce_over_bl(partial, bl_devices):
     bits = bl_devices.bit_length() - 1
     rows = partial.shape[0]
@@ -53,7 +79,12 @@
             keep = lax.index_in_dim(parts[p], 0, axis, keepdims=False)
             send = lax.index_in_dim(parts[p], 1, axis, keepdims=False)
             pairs = [(q, q ^ (1 << bit)) for q in range(bl_devices)]
-            parts[p] = keep + lax.ppermute(send, "bl", perm=pairs)
+            row_axis = len(axis_bits[p]) - 1
+            if send.shape[row_axis] % 2 == 0:
+                moved = lax.ppermute(encode_pairs(send, row_axis), "bl", perm=pairs)
+                parts[p] = keep + decode_pairs(moved, row_axis)
+            else:
+                parts[p] = keep + lax.ppermute(send, "bl", perm=pairs)
             axis_bits[p].pop(axis)
     return jnp.concatenate(parts, axis=2)
 

time: 336 us -> 358 us (1.065)
  other arithmetic: 21 us -> 41.5 us
  local copies, waits for them, and re-layouts: 44.5 us -> 51.8 us
  matrix products: 85.1 us -> 79.3 us
    all_to_all x3, waiting for transfers between devices: 16.6 us -> 27.9 us  [body(): lax.all_to_all(summed_modes, 'freq', split_axis=0, concat_axis=1, tiled=T...]
    ppermute x16, waiting for transfers between devices: 96.8 us -> 87.7 us  [reduce_over_bl(): moved = lax.ppermute(encode_pairs(send, row_axis), 'bl', perm=pairs)]
    squeeze x16 -> x0, local copies, waits for them, and re-layouts: 8.69 us -> none  [reduce_over_bl(): send = lax.index_in_dim(parts[p], 1, axis, keepdims=False)]
    all_to_all x4 -> x8, local copies, waits for them, and re-layouts: 1.54 us -> 9.99 us  [body(): lax.all_to_all(summed_modes, 'freq', split_axis=0, concat_axis=1, tiled=T...]
    concatenate x0 -> x32, other arithmetic: none -> 6.71 us  [encode_pairs(): return jnp.concatenate([high, code], axis=axis).astype(jnp.bfloat16)]
    round x0 -> x16, other arithmetic: none -> 6.1 us  [decode_pairs(): first = jnp.round(code / (2 * RESIDUAL_LEVELS + 1))]
    dot_general x4, matrix products: 16.3 us -> 11.2 us  [project(): lax.dot_general(low, beam_rows, dims, preferred_element_type=jnp.float32)]
    unnamed x25 -> x35, local copies, waits for them, and re-layouts: 8.36 us -> 12.1 us
  transfers between devices with their start and end apart: 19 -> 19, of which waited for: 13 -> 10; matrix products, arithmetic and copies ran while one was open for 19% -> 21% of each run, Pallas kernels for 0% -> 0%
where the time goes in v2:
time: 358 us; the launch traced here: 352 us
  waiting for transfers between devices  116 us (32%)
  matrix products  79.3 us (22%)
  local copies, waits for them, and re-layouts  51.8 us (14%)
  other arithmetic  41.5 us (12%)
  starting transfers between devices  33.2 us (9%)
  blocking collectives  29 us (8%)
    ppermute x16, waiting for transfers between devices, reduce_over_bl(): moved = lax.ppermute(encode_pairs(send, row_axis), 'bl', perm=pairs)  87.7 us
    dot_general x4, matrix products, weigh_all(): jnp.einsum('mfg,mgcs->mfcs', inverse_cov, owner_modes, precision=lax.Prec...  32.9 us
    all_to_all x1, blocking collectives, body(): lax.all_to_all(summed_modes, 'freq', split_axis=0, concat_axis=1, tiled=T...  29 us
    all_to_all x3, waiting for transfers between devices, body(): lax.all_to_all(summed_modes, 'freq', split_axis=0, concat_axis=1, tiled=T...  27.9 us
    dot_general x1, matrix products, transform(): lax.dot_general(samples, dft_weights, (((0, 3), (0, 1)), ((), ())), prefe...  24 us
    ppermute x16, starting transfers between devices, reduce_over_bl(): moved = lax.ppermute(encode_pairs(send, row_axis), 'bl', perm=pairs)  19.4 us
    all_to_all x3, starting transfers between devices, body(): lax.all_to_all(summed_modes, 'freq', split_axis=0, concat_axis=1, tiled=T...  13.8 us
    slice x1, local copies, waits for them, and re-layouts, body(): spectrum[:, :, step * width:(step + 1) * width]  12.5 us
  transfers between devices with their start and end apart: 19, of which 10 were waited for; matrix products, arithmetic and copies ran while one was open for 21% of the time, Pallas kernels for 0%

profile of v2, /device:TPU:0, one launch (start us, length us, event | category | flops | bytes accessed | tf_op | source)
XLA Modules:
  0.0 351.8 jit_solution(6821513400600821677)
XLA Ops:
  1.9 4.6 %negate_convert_fusion = (bf16[1024,4,1,64]{0,3,2,1:T(8,128)(2,1)S(1)}, bf16[1024,4,1,64]{0,3,2,1:T(8,128)(2,1)S(1)}, bf16[1024,4,1,64]{0,3,2,1:T(8,128)(2,1)S(1)}) fusion(s32[1024]{0:T(1024)S(1)} %iota_add_fusion, s32[4,64]{1,0:T(4,128)S(1)} %copy.158), kind=kLoop, calls=%fused_computation.255 | loop fusion | flops 5242880 | bytes 1577984 | tf_op jit(solution)/shard_map/convert.55
  6.7 24.0 %convolution_bitcast_fusion = f32[64,128,512]{1,2,0:T(8,128)} fusion(bf16[2,64,128,1024]{3,2,1,0:T(8,128)(2,1)} %param.5, bf16[1,1024,512]{1,2,0:T(8,128)(2,1)S(1)} %bitcast.874, bf16[1,1024,512]{1,2,0:T(8,128)(2,1)S(1)} %bitcast.873), kind=kOutput, calls=%fused_computation.2 | convolution fusion | flops 17184063488 | bytes 52428800 | tf_op jit(solution)/shard_map/dot_general | solution.py:24
  30.7 12.5 %fusion.236 = (f32[64,128,128]{1,2,0:T(8,128)}, f32[64,128,128]{1,2,0:T(8,128)}, f32[64,128,128]{1,2,0:T(8,128)}, f32[64,128,128]{1,2,0:T(8,128)}) fusion(f32[64,128,512]{1,2,0:T(8,128)} %convolution_bitcast_fusion), kind=kLoop, calls=%fused_computation.499 | loop fusion | bytes 33554432 | tf_op jit(solution)/shard_map/slice | solution.py:120
  43.2 6.8 %copy.161 = bf16[256,64,64]{2,1,0:T(8,128)(2,1)} copy(bf16[256,64,64]{0,2,1:T(8,128)(2,1)S(1)} %copy-done.11) | data formatting | bytes 4194304 | tf_op args[2]
  50.0 5.4 %gather_fusion.1 = bf16[4,8,4,2,64,64]{5,4,3,2,1,0:T(8,128)(2,1)} fusion(bf16[4,8,4,2,64,64]{5,4,3,2,1,0:T(8,128)(2,1)} %bitcast.855, s32[1024]{0:T(1024)} %copy-done.14), kind=kCustom, calls=%fused_computation.1 | custom fusion | bytes 4194320 | tf_op jit(solution)/shard_map/jit(_take)/gather | solution.py:111
  55.4 2.7 broadcast_select_fusion
  58.1 1.8 fusion.237
  60.3 2.8 fusion.21
  63.0 2.7 convolution_add_fusion.2
  66.7 3.0 collective-permute-start.6
  70.0 1.6 collective-permute-start.4
  71.6 2.8 fusion.20
  74.3 3.1 convolution_add_fusion.3
  78.7 2.5 copy-done.1
  81.1 2.8 fusion.22
  83.9 2.7 convolution_add_fusion.1
  87.8 2.5 copy-done
  90.3 2.8 fusion.23
  93.1 2.8 convolution_add_fusion
  98.3 9.1 %collective-permute-done = bf16[2,24,128,1,64]{2,4,1,3,0:T(8,128)(2,1)S(1)} collective-permute-done((bf16[2,24,128,1,64]{2,4,1,3,0:T(8,128)(2,1)S(1)}, bf16[2,24,128,1,64]{2,4,1,3,0:T(8,128)(2,1)S(1)}, u32[]{:S(2)}, u32[]{:S(2)}) %collective-permute-start) | collective-permute-done | bytes 786464 | tf_op jit(solution)/shard_map/ppermute | solution.py:84
  109.2 15.0 %collective-permute-done.8 = bf16[2,24,128,1,64]{2,4,1,3,0:T(8,128)(2,1)S(1)} collective-permute-done((bf16[2,24,128,1,64]{2,4,1,3,0:T(8,128)(2,1)S(1)}, bf16[2,24,128,1,64]{2,4,1,3,0:T(8,128)(2,1)S(1)}, u32[]{:S(2)}, u32[]{:S(2)}) %collective-permute-start.8) | collective-permute-done | bytes 786464 | tf_op jit(solution)/shard_map/ppermute | solution.py:84
  125.7 13.9 %collective-permute-done.12 = bf16[2,24,128,1,64]{2,4,1,0,3:T(8,128)(2,1)S(1)} collective-permute-done((bf16[2,24,128,1,64]{2,4,1,0,3:T(8,128)(2,1)S(1)}, bf16[2,24,128,1,64]{2,4,1,0,3:T(8,128)(2,1)S(1)}, u32[]{:S(2)}, u32[]{:S(2)}) %collective-permute-start.12) | collective-permute-done | bytes 786464 | tf_op jit(solution)/shard_map/ppermute | solution.py:84
  141.1 1.8 collective-permute-start.7
  143.7 1.5 collective-permute-start.1
  147.6 1.5 collective-permute-start.9
  149.3 1.0 pad_maximum_fusion.12
  151.1 1.0 maximum_bitcast_fusion.1
  153.2 1.8 collective-permute-start.13
  155.3 1.0 pad_maximum_fusion.4
  156.3 5.1 %all-to-all-start = ((f32[16,128,2,64]{1,3,2,0:T(8,128)}), f32[16,128,2,64]{1,3,2,0:T(8,128)}, u32[]{:S(2)}, u32[]{:S(2)}) async-start(f32[16,128,2,64]{1,3,2,0:T(8,128)} %pad_maximum_fusion.4), calls=%async_computation | async-start | bytes 2097152 | tf_op jit(solution)/shard_map/all_to_all | solution.py:124
  163.0 23.6 %collective-permute-done.9 = bf16[24,128,1,64]{1,3,0,2:T(8,128)(2,1)} collective-permute-done((bf16[24,128,1,64]{1,3,0,2:T(8,128)(2,1)}, bf16[24,128,1,64]{1,3,0,2:T(8,128)(2,1)}, u32[]{:S(2)}, u32[]{:S(2)}) %collective-permute-start.9) | collective-permute-done | bytes 393248 | tf_op jit(solution)/shard_map/ppermute | solution.py:84
  187.6 1.1 fusion.128
  188.6 1.9 fusion.142
  190.5 1.1 fusion.129
  191.6 1.6 fusion.67
  193.6 1.6 collective-permute-start.3
  195.1 8.3 %collective-permute-done.10 = bf16[2,24,128,1,64]{2,4,1,0,3:T(8,128)(2,1)} collective-permute-done((bf16[2,24,128,1,64]{2,4,1,0,3:T(8,128)(2,1)}, bf16[2,24,128,1,64]{2,4,1,0,3:T(8,128)(2,1)}, u32[]{:S(2)}, u32[]{:S(2)}) %collective-permute-start.10) | collective-permute-done | bytes 786464 | tf_op jit(solution)/shard_map/ppermute | solution.py:84
  203.5 1.1 fusion.143
  204.5 1.6 fusion.75
  206.4 1.1 pad_maximum_fusion.3
  207.4 2.9 copy.342
  210.3 1.4 all_to_all.55
  211.7 8.8 %fusion.34 = f32[2,1024,2,64]{1,3,2,0:T(8,128)} fusion(f32[2,1024,2,64]{1,3,2,0:T(8,128)S(1)} %all_to_all.55, f32[8,1024,1024]{2,1,0:T(8,128)} %param.8, f32[2,1024]{1,0:T(2,128)} %get-tuple-element.71), kind=kOutput, calls=%fused_computation.121 | convolution fusion | flops 1611137024 | bytes 11542528 | tf_op jit(solution)/shard_map/mfg,mgcs->mfcs/dot_general | solution.py:93
  220.5 1.1 copy.258
  221.6 4.9 %all-to-all-start.1 = ((f32[16,128,2,64]{1,3,2,0:T(8,128)}), f32[16,128,2,64]{1,3,2,0:T(8,128)}, u32[]{:S(2)}, u32[]{:S(2)}) async-start(f32[16,128,2,64]{1,3,2,0:T(8,128)} %copy.258), calls=%async_computation.1 | async-start | bytes 2097152 | tf_op jit(solution)/shard_map/all_to_all | solution.py:124
  226.8 1.6 collective-permute-start.11
  228.4 1.1 fusion.151
  229.4 1.6 fusion.81
  231.1 7.3 %collective-permute-done.11 = bf16[24,128,1,64]{1,3,0,2:T(8,128)(2,1)S(1)} collective-permute-done((bf16[24,128,1,64]{1,3,0,2:T(8,128)(2,1)S(1)}, bf16[24,128,1,64]{1,3,0,2:T(8,128)(2,1)S(1)}, u32[]{:S(2)}, u32[]{:S(2)}) %collective-permute-start.11) | collective-permute-done | bytes 393248 | tf_op jit(solution)/shard_map/ppermute | solution.py:84
  238.6 1.1 pad_maximum_fusion.5
  239.7 13.5 %all-to-all-done.1 = f32[16,128,2,64]{1,3,2,0:T(8,128)} async-done(((f32[16,128,2,64]{1,3,2,0:T(8,128)}), f32[16,128,2,64]{1,3,2,0:T(8,128)}, u32[]{:S(2)}, u32[]{:S(2)}) %all-to-all-start.1) | async-done | bytes 1048608 | tf_op jit(solution)/shard_map/all_to_all | solution.py:124
  253.2 2.8 copy.341
  256.0 1.4 all_to_all.59
  257.4 8.7 %fusion.43 = f32[2,1024,2,64]{1,3,2,0:T(8,128)} fusion(f32[2,1024,2,64]{1,3,2,0:T(8,128)S(1)} %all_to_all.59, f32[8,1024,1024]{2,1,0:T(8,128)} %param.8, f32[2,1024]{1,0:T(2,128)} %get-tuple-element.70), kind=kOutput, calls=%fused_computation.124 | convolution fusion | flops 1611137024 | bytes 11542528 | tf_op jit(solution)/shard_map/mfg,mgcs->mfcs/dot_general | solution.py:93
  266.1 1.1 copy.290
  267.2 3.8 %all-to-all-start.2 = ((f32[16,128,2,64]{1,3,2,0:T(8,128)}), f32[16,128,2,64]{1,3,2,0:T(8,128)S(1)}, u32[]{:S(2)}, u32[]{:S(2)}) async-start(f32[16,128,2,64]{1,3,2,0:T(8,128)} %copy.290), calls=%async_computation.2 | async-start | bytes 2097152 | tf_op jit(solution)/shard_map/all_to_all | solution.py:124
  271.4 1.6 collective-permute-start.15
  273.1 9.8 %collective-permute-done.15 = bf16[24,128,1,64]{1,3,0,2:T(8,128)(2,1)S(1)} collective-permute-done((bf16[24,128,1,64]{1,3,0,2:T(8,128)(2,1)S(1)}, bf16[24,128,1,64]{1,3,0,2:T(8,128)(2,1)S(1)}, u32[]{:S(2)}, u32[]{:S(2)}) %collective-permute-start.15) | collective-permute-done | bytes 393248 | tf_op jit(solution)/shard_map/ppermute | solution.py:84
  283.1 14.4 %all-to-all-done.2 = f32[16,128,2,64]{1,3,2,0:T(8,128)S(1)} async-done(((f32[16,128,2,64]{1,3,2,0:T(8,128)}), f32[16,128,2,64]{1,3,2,0:T(8,128)S(1)}, u32[]{:S(2)}, u32[]{:S(2)}) %all-to-all-start.2) | async-done | bytes 1048608 | tf_op jit(solution)/shard_map/all_to_all | solution.py:124
  298.3 7.6 %fusion.52 = f32[2,1024,2,64]{1,3,2,0:T(8,128)S(1)} fusion(f32[2,1024,2,64]{1,3,2,0:T(8,128)S(1)} %all_to_all.63, f32[8,1024,1024]{2,1,0:T(8,128)} %param.8, f32[2,1024]{1,0:T(2,128)S(1)} %get-tuple-element.72), kind=kOutput, calls=%fused_computation.127 | convolution fusion | flops 1611137024 | bytes 11542528 | tf_op jit(solution)/shard_map/mfg,mgcs->mfcs/dot_general | solution.py:93
  306.0 29.0 %all_to_all.72 = f32[16,128,2,64]{1,3,2,0:T(8,128)S(1)} all-to-all(f32[16,128,2,64]{1,3,2,0:T(8,128)S(1)} %pad_maximum_fusion.6), channel_id=1, replica_groups=mesh['bl'=4,'freq'=8] {'freq'}, dimensions={0} | all-to-all | bytes 2097152 | tf_op jit(solution)/shard_map/all_to_all | solution.py:124
  335.8 7.8 %fusion.61 = f32[2,1024,2,64]{1,3,2,0:T(8,128)S(1)} fusion(f32[2,1024,2,64]{1,3,2,0:T(8,128)S(1)} %all_to_all.67, f32[8,1024,1024]{2,1,0:T(8,128)} %param.8, f32[2,1024]{1,0:T(2,128)S(1)} %get-tuple-element.69), kind=kOutput, calls=%fused_computation.130 | convolution fusion | flops 1611137024 | bytes 11542528 | tf_op jit(solution)/shard_map/mfg,mgcs->mfcs/dot_general | solution.py:93
  343.6 2.4 pad_maximum_fusion
  346.0 5.3 %copy.293 = f32[8,1024,128]{2,1,0:T(8,128)} copy(f32[8,1024,128]{1,2,0:T(8,128)} %bitcast.854) | data formatting | bytes 8388608 | tf_op jit(solution)/shard_map/reshape | solution.py:130
  (147 shorter events, 24.3 us)
Async XLA Ops:
  0.0 6.7 %copy-start.15 = (pred[4]{0:T(512)(128)(4,1)}, pred[4]{0:T(512)(128)(4,1)S(1)}, u32[]{:S(2)}) copy-start(pred[4]{0:T(512)(128)(4,1)S(1)} %compare_and_fusion) | copy-start | bytes 16
  0.0 6.7 %copy-start.14 = (s32[1024]{0:T(1024)}, s32[1024]{0:T(1024)S(1)}, u32[]{:S(2)}) copy-start(s32[1024]{0:T(1024)S(1)} %pad_clamp_fusion) | copy-start | bytes 12292
  30.7 12.5 %copy-start.11 = (bf16[256,64,64]{0,2,1:T(8,128)(2,1)S(1)}, bf16[256,64,64]{0,2,1:T(8,128)(2,1)}, u32[]{:S(2)}) copy-start(bf16[256,64,64]{0,2,1:T(8,128)(2,1)} %param.7) | copy-start | bytes 6291460
  50.0 5.4 %copy-start.16 = (pred[4]{0:T(512)(128)(4,1)S(1)}, pred[4]{0:T(512)(128)(4,1)}, u32[]{:S(2)}) copy-start(pred[4]{0:T(512)(128)(4,1)} %copy-done.15) | copy-start | bytes 16
  58.1 2.2 copy-start.3
  66.5 5.1 %copy-start.2 = (f32[64,128,128]{1,2,0:T(8,128)S(1)}, f32[64,128,128]{1,2,0:T(8,128)}, u32[]{:S(2)}) copy-start(f32[64,128,128]{1,2,0:T(8,128)} %get-tuple-element.20) | copy-start | bytes 12582916
  66.7 31.3 %collective-permute-start.6 = (bf16[2,24,128,1,64]{2,4,1,0,3:T(8,128)(2,1)S(1)}, bf16[2,24,128,1,64]{2,4,1,0,3:T(8,128)(2,1)S(1)}, u32[]{:S(2)}, u32[]{:S(2)}) collective-permute-start(bf16[2,24,128,1,64]{2,4,1,0,3:T(8,128)(2,1)S(1)} %pad_maximum_fusion.10), channel_id=1, source_target_pairs={{0,16},{8,24},{16,0},{24,8},{1,17},{9,25},{17,1},{25,9},{2,18},{10... | collective-permute-start | bytes 2359304 | tf_op jit(solution)/shard_map/ppermute | solution.py:84
  70.0 28.2 %collective-permute-start.4 = (bf16[2,24,128,1,64]{2,4,1,0,3:T(8,128)(2,1)S(1)}, bf16[2,24,128,1,64]{2,4,1,0,3:T(8,128)(2,1)S(1)}, u32[]{:S(2)}, u32[]{:S(2)}) collective-permute-start(bf16[2,24,128,1,64]{2,4,1,0,3:T(8,128)(2,1)S(1)} %pad_maximum_fusion.9), channel_id=1, source_target_pairs={{0,8},{8,0},{16,24},{24,16},{1,9},{9,1},{17,25},{25,17},{2,10},{10... | collective-permute-start | bytes 2359304 | tf_op jit(solution)/shard_map/ppermute | solution.py:84
  77.4 30.1 %copy-start.6 = (f32[64,128,2,64]{1,3,2,0:T(8,128)}, f32[64,128,2,64]{1,3,2,0:T(8,128)S(1)}, u32[]{:S(2)}) copy-start(f32[64,128,2,64]{1,3,2,0:T(8,128)S(1)} %convolution_add_fusion.3) | copy-start | bytes 12582916
  77.4 3.7 %copy-start.1 = (f32[64,128,128]{1,2,0:T(8,128)S(1)}, f32[64,128,128]{1,2,0:T(8,128)}, u32[]{:S(2)}) copy-start(f32[64,128,128]{1,2,0:T(8,128)} %get-tuple-element.19) | copy-start | bytes 12582916
  78.1 29.3 %collective-permute-start = (bf16[2,24,128,1,64]{2,4,1,3,0:T(8,128)(2,1)S(1)}, bf16[2,24,128,1,64]{2,4,1,3,0:T(8,128)(2,1)S(1)}, u32[]{:S(2)}, u32[]{:S(2)}) collective-permute-start(bf16[2,24,128,1,64]{2,4,1,3,0:T(8,128)(2,1)S(1)} %pad_maximum_fusion.7), channel_id=1, source_target_pairs={{0,8},{8,0},{16,24},{24,16},{1,9},{9,1},{17,25},{25,17},{2,10},{10... | collective-permute-start | bytes 2359304 | tf_op jit(solution)/shard_map/ppermute | solution.py:84
  86.6 37.8 %copy-start.5 = (f32[64,128,2,64]{1,3,2,0:T(8,128)}, f32[64,128,2,64]{1,3,2,0:T(8,128)S(1)}, u32[]{:S(2)}) copy-start(f32[64,128,2,64]{1,3,2,0:T(8,128)S(1)} %convolution_add_fusion.1) | copy-start | bytes 12582916
  86.6 3.7 %copy-start = (f32[64,128,128]{1,2,0:T(8,128)S(1)}, f32[64,128,128]{1,2,0:T(8,128)}, u32[]{:S(2)}) copy-start(f32[64,128,128]{1,2,0:T(8,128)} %get-tuple-element.18) | copy-start | bytes 12582916
  87.2 37.0 %collective-permute-start.8 = (bf16[2,24,128,1,64]{2,4,1,3,0:T(8,128)(2,1)S(1)}, bf16[2,24,128,1,64]{2,4,1,3,0:T(8,128)(2,1)S(1)}, u32[]{:S(2)}, u32[]{:S(2)}) collective-permute-start(bf16[2,24,128,1,64]{2,4,1,3,0:T(8,128)(2,1)S(1)} %pad_maximum_fusion.11), channel_id=1, source_target_pairs={{0,8},{8,0},{16,24},{24,16},{1,9},{9,1},{17,25},{25,17},{2,10},{10... | collective-permute-start | bytes 2359304 | tf_op jit(solution)/shard_map/ppermute | solution.py:84
  95.9 43.8 %copy-start.4 = (f32[64,128,2,64]{1,3,2,0:T(8,128)}, f32[64,128,2,64]{1,3,2,0:T(8,128)S(1)}, u32[]{:S(2)}) copy-start(f32[64,128,2,64]{1,3,2,0:T(8,128)S(1)} %convolution_add_fusion) | copy-start | bytes 12582916
  96.3 1.0 copy-start.13
  96.6 43.1 %collective-permute-start.12 = (bf16[2,24,128,1,64]{2,4,1,0,3:T(8,128)(2,1)S(1)}, bf16[2,24,128,1,64]{2,4,1,0,3:T(8,128)(2,1)S(1)}, u32[]{:S(2)}, u32[]{:S(2)}) collective-permute-start(bf16[2,24,128,1,64]{2,4,1,0,3:T(8,128)(2,1)S(1)} %pad_maximum_fusion.13), channel_id=1, source_target_pairs={{0,8},{8,0},{16,24},{24,16},{1,9},{9,1},{17,25},{25,17},{2,10},{10... | collective-permute-start | bytes 2359304 | tf_op jit(solution)/shard_map/ppermute | solution.py:84
  140.7 12.1 %collective-permute-start.5 = (bf16[24,128,1,64]{1,3,0,2:T(8,128)(2,1)S(1)}, bf16[24,128,1,64]{1,3,0,2:T(8,128)(2,1)S(1)}, u32[]{:S(2)}, u32[]{:S(2)}) collective-permute-start(bf16[24,128,1,64]{1,3,0,2:T(8,128)(2,1)S(1)} %pad_maximum_fusion.16), channel_id=1, source_target_pairs={{0,16},{8,24},{16,0},{24,8},{1,17},{9,25},{17,1},{25,9},{2,18},{10... | collective-permute-start | bytes 1179656 | tf_op jit(solution)/shard_map/ppermute | solution.py:84
  141.1 12.0 %collective-permute-start.7 = (bf16[24,128,1,64]{1,3,0,2:T(8,128)(2,1)S(1)}, bf16[24,128,1,64]{1,3,0,2:T(8,128)(2,1)S(1)}, u32[]{:S(2)}, u32[]{:S(2)}) collective-permute-start(bf16[24,128,1,64]{1,3,0,2:T(8,128)(2,1)S(1)} %pad_maximum_fusion.17), channel_id=1, source_target_pairs={{0,8},{8,0},{16,24},{24,16},{1,9},{9,1},{17,25},{25,17},{2,10},{10... | collective-permute-start | bytes 1179656 | tf_op jit(solution)/shard_map/ppermute | solution.py:84
  143.7 17.8 %collective-permute-start.1 = (bf16[24,128,1,64]{1,3,0,2:T(8,128)(2,1)}, bf16[24,128,1,64]{1,3,0,2:T(8,128)(2,1)}, u32[]{:S(2)}, u32[]{:S(2)}) collective-permute-start(bf16[24,128,1,64]{1,3,0,2:T(8,128)(2,1)} %pad_maximum_fusion.14), channel_id=1, source_target_pairs={{0,16},{8,24},{16,0},{24,8},{1,17},{9,25},{17,1},{25,9},{2,18},{10... | collective-permute-start | bytes 1179656 | tf_op jit(solution)/shard_map/ppermute | solution.py:84
  146.3 44.2 %collective-permute-start.2 = (bf16[2,24,128,1,64]{2,4,1,0,3:T(8,128)(2,1)}, bf16[2,24,128,1,64]{2,4,1,0,3:T(8,128)(2,1)}, u32[]{:S(2)}, u32[]{:S(2)}) collective-permute-start(bf16[2,24,128,1,64]{2,4,1,0,3:T(8,128)(2,1)} %pad_maximum_fusion.8), channel_id=1, source_target_pairs={{0,16},{8,24},{16,0},{24,8},{1,17},{9,25},{17,1},{25,9},{2,18},{10... | collective-permute-start | bytes 2359304 | tf_op jit(solution)/shard_map/ppermute | solution.py:84
  147.6 39.0 %collective-permute-start.9 = (bf16[24,128,1,64]{1,3,0,2:T(8,128)(2,1)}, bf16[24,128,1,64]{1,3,0,2:T(8,128)(2,1)}, u32[]{:S(2)}, u32[]{:S(2)}) collective-permute-start(bf16[24,128,1,64]{1,3,0,2:T(8,128)(2,1)} %pad_maximum_fusion.18), channel_id=1, source_target_pairs={{0,16},{8,24},{16,0},{24,8},{1,17},{9,25},{17,1},{25,9},{2,18},{10... | collective-permute-start | bytes 1179656 | tf_op jit(solution)/shard_map/ppermute | solution.py:84
  152.8 50.7 %collective-permute-start.10 = (bf16[2,24,128,1,64]{2,4,1,0,3:T(8,128)(2,1)}, bf16[2,24,128,1,64]{2,4,1,0,3:T(8,128)(2,1)}, u32[]{:S(2)}, u32[]{:S(2)}) collective-permute-start(bf16[2,24,128,1,64]{2,4,1,0,3:T(8,128)(2,1)} %pad_maximum_fusion.12), channel_id=1, source_target_pairs={{0,16},{8,24},{16,0},{24,8},{1,17},{9,25},{17,1},{25,9},{2,18},{10... | collective-permute-start | bytes 2359304 | tf_op jit(solution)/shard_map/ppermute | solution.py:84
  153.2 119.7 %collective-permute-start.13 = (bf16[24,128,1,64]{1,3,2,0:T(8,128)(2,1)}, bf16[24,128,1,64]{1,3,2,0:T(8,128)(2,1)S(1)}, u32[]{:S(2)}, u32[]{:S(2)}) collective-permute-start(bf16[24,128,1,64]{1,3,2,0:T(8,128)(2,1)} %pad_maximum_fusion.20), channel_id=1, source_target_pairs={{0,16},{8,24},{16,0},{24,8},{1,17},{9,25},{17,1},{25,9},{2,18},{10... | collective-permute-start | bytes 1179656 | tf_op jit(solution)/shard_map/ppermute | solution.py:84
  156.3 51.1 %all-to-all-start = ((f32[16,128,2,64]{1,3,2,0:T(8,128)}), f32[16,128,2,64]{1,3,2,0:T(8,128)}, u32[]{:S(2)}, u32[]{:S(2)}) async-start(f32[16,128,2,64]{1,3,2,0:T(8,128)} %pad_maximum_fusion.4), calls=%async_computation | async-start | bytes 2097152 | tf_op jit(solution)/shard_map/all_to_all | solution.py:124
  161.5 66.9 %collective-permute-start.14 = (bf16[2,24,128,1,64]{2,4,1,3,0:T(8,128)(2,1)}, bf16[2,24,128,1,64]{2,4,1,3,0:T(8,128)(2,1)}, u32[]{:S(2)}, u32[]{:S(2)}) collective-permute-start(bf16[2,24,128,1,64]{2,4,1,3,0:T(8,128)(2,1)} %maximum_bitcast_fusion.1), channel_id=1, source_target_pairs={{0,16},{8,24},{16,0},{24,8},{1,17},{9,25},{17,1},{25,9},{2,18},{10... | collective-permute-start | bytes 2359304 | tf_op jit(solution)/shard_map/ppermute | solution.py:84
  193.6 12.6 %collective-permute-start.3 = (bf16[24,128,1,64]{1,3,0,2:T(8,128)(2,1)S(1)}, bf16[24,128,1,64]{1,3,0,2:T(8,128)(2,1)S(1)}, u32[]{:S(2)}, u32[]{:S(2)}) collective-permute-start(bf16[24,128,1,64]{1,3,0,2:T(8,128)(2,1)S(1)} %pad_maximum_fusion.15), channel_id=1, source_target_pairs={{0,8},{8,0},{16,24},{24,16},{1,9},{9,1},{17,25},{25,17},{2,10},{10... | collective-permute-start | bytes 1179656 | tf_op jit(solution)/shard_map/ppermute | solution.py:84
  211.7 8.8 %copy-start.7 = (f32[16,128,2,64]{1,3,0,2:T(8,128)S(1)}, f32[16,128,2,64]{1,3,0,2:T(8,128)}, u32[]{:S(2)}) copy-start(f32[16,128,2,64]{1,3,0,2:T(8,128)} %pad_maximum_fusion.3) | copy-start | bytes 3145732
  221.6 31.6 %all-to-all-start.1 = ((f32[16,128,2,64]{1,3,2,0:T(8,128)}), f32[16,128,2,64]{1,3,2,0:T(8,128)}, u32[]{:S(2)}, u32[]{:S(2)}) async-start(f32[16,128,2,64]{1,3,2,0:T(8,128)} %copy.258), calls=%async_computation.1 | async-start | bytes 2097152 | tf_op jit(solution)/shard_map/all_to_all | solution.py:124
  226.7 11.8 %copy-start.12 = (f32[16,128,1,64]{1,3,0,2:T(8,128)S(1)}, f32[16,128,1,64]{1,3,0,2:T(8,128)}, u32[]{:S(2)}) copy-start(f32[16,128,1,64]{1,3,0,2:T(8,128)} %fusion.142) | copy-start | bytes 1572868
  226.8 11.6 %collective-permute-start.11 = (bf16[24,128,1,64]{1,3,0,2:T(8,128)(2,1)S(1)}, bf16[24,128,1,64]{1,3,0,2:T(8,128)(2,1)S(1)}, u32[]{:S(2)}, u32[]{:S(2)}) collective-permute-start(bf16[24,128,1,64]{1,3,0,2:T(8,128)(2,1)S(1)} %pad_maximum_fusion.19), channel_id=1, source_target_pairs={{0,8},{8,0},{16,24},{24,16},{1,9},{9,1},{17,25},{25,17},{2,10},{10... | collective-permute-start | bytes 1179656 | tf_op jit(solution)/shard_map/ppermute | solution.py:84
  257.4 8.7 %copy-start.8 = (f32[16,128,2,64]{1,3,0,2:T(8,128)S(1)}, f32[16,128,2,64]{1,3,0,2:T(8,128)}, u32[]{:S(2)}) copy-start(f32[16,128,2,64]{1,3,0,2:T(8,128)} %pad_maximum_fusion.5) | copy-start | bytes 3145732
  267.2 30.3 %all-to-all-start.2 = ((f32[16,128,2,64]{1,3,2,0:T(8,128)}), f32[16,128,2,64]{1,3,2,0:T(8,128)S(1)}, u32[]{:S(2)}, u32[]{:S(2)}) async-start(f32[16,128,2,64]{1,3,2,0:T(8,128)} %copy.290), calls=%async_computation.2 | async-start | bytes 2097152 | tf_op jit(solution)/shard_map/all_to_all | solution.py:124
  271.4 11.5 %collective-permute-start.15 = (bf16[24,128,1,64]{1,3,0,2:T(8,128)(2,1)S(1)}, bf16[24,128,1,64]{1,3,0,2:T(8,128)(2,1)S(1)}, u32[]{:S(2)}, u32[]{:S(2)}) collective-permute-start(bf16[24,128,1,64]{1,3,0,2:T(8,128)(2,1)S(1)} %pad_maximum_fusion.21), channel_id=1, source_target_pairs={{0,8},{8,0},{16,24},{24,16},{1,9},{9,1},{17,25},{25,17},{2,10},{10... | collective-permute-start | bytes 1179656 | tf_op jit(solution)/shard_map/ppermute | solution.py:84
  335.7 7.8 %copy-start.9 = (f32[2,1024,2,64]{1,3,2,0:T(8,128)S(1)}, f32[2,1024,2,64]{1,3,2,0:T(8,128)}, u32[]{:S(2)}) copy-start(f32[2,1024,2,64]{1,3,2,0:T(8,128)} %fusion.34) | copy-start | bytes 3145732
  335.8 7.8 %copy-start.10 = (f32[2,1024,2,64]{1,3,2,0:T(8,128)S(1)}, f32[2,1024,2,64]{1,3,2,0:T(8,128)}, u32[]{:S(2)}) copy-start(f32[2,1024,2,64]{1,3,2,0:T(8,128)} %fusion.43) | copy-start | bytes 3145732
